TPU v7x, 512 devices: a whole 4x4x16 slice. The times are simulated.
512 devices in a mesh: pipe: 8 (over y, x_lo), expert: 64 (over x_hi, z, core).
Axes of the slice: x: 4 (x_hi: 2, x_lo: 2; x = x_hi * 2 + x_lo), y: 4, z: 16, core: 2. Of those that a mesh axis runs over, the one named last changes fastest.
Arguments:
- fwd_tokens: bfloat16 [8, 1024, 3584], P('pipe', 'expert'), may hold values from -6 to 6
- fwd_routes: int32 [8, 1024, 2], P('pipe', 'expert'), may hold values from 0 to 7, all different within a row; in each aligned block of 16 rows (0 to 15, 16 to 31, ..., all dimensions but the last counted through in order) at most 6 rows name the same one
- fwd_scores: float32 [8, 1024, 2], P('pipe', 'expert'), may hold values from 0.1 to 1
- bwd_tokens: bfloat16 [8, 1024, 3584], P('pipe', 'expert'), may hold values from -6 to 6
- bwd_routes: int32 [8, 1024, 2], P('pipe', 'expert'), may hold values from 0 to 7, all different within a row; in each aligned block of 16 rows (0 to 15, 16 to 31, ..., all dimensions but the last counted through in order) at most 6 rows name the same one
- bwd_scores: float32 [8, 1024, 2], P('pipe', 'expert'), may hold values from 0.1 to 1
- out_grad: bfloat16 [8, 1024, 3584], P('pipe', 'expert'), may hold values from -6 to 6
- gate_weight: bfloat16 [8, 3584, 8192], P('pipe', None, 'expert'), may hold values from -0.09375 to 0.09375
- up_weight: bfloat16 [8, 3584, 8192], P('pipe', None, 'expert'), may hold values from -0.09375 to 0.09375
- down_weight: bfloat16 [8, 8192, 3584], P('pipe', 'expert'), may hold values from -0.1875 to 0.1875
Outputs:
- next_input: bfloat16 [8, 1024, 3584], P('pipe', 'expert')
- prev_grad: bfloat16 [8, 1024, 3584], P('pipe', 'expert')
Inputs may be any that keep to these rules, and one draw needn't show every extreme that they name: `fwd_routes`: each row names 2 different experts. Among the 16 rows of one device in one section, no expert is named more than 6 times, a bound that some block reaches. `bwd_routes`: each row names 2 different experts. Among the 16 rows of one device in one section, no expert is named more than 6 times, a bound that some block reaches.
All inputs are finite; a program needn't handle non-finite values.
Results may differ from a plain program's by a relative error of at most 0.011.
Values may be sent and summed in bfloat16 or wider, within the bound.
No kernel may reach another device: no remote copies, remote signals or barrier semaphores. Data moves between devices by JAX's collectives and lax.ppermute only.
A program may use at most 128 MiB of HBM per device.

v0:
```python
import jax
import jax.numpy as jnp
from jax import lax
from jax.sharding import PartitionSpec as P

GROUP = 8


def from_behind(value, axis, steps):
    count = lax.axis_size(axis)
    pairs = [(source, (source + steps) % count) for source in range(count)]
    return lax.ppermute(value, axis, pairs)


def route_tables(routes, scores, capacity, experts):
    tokens, topk = routes.shape
    flat = routes.reshape(-1)
    onehot = (flat[:, None] == jnp.arange(experts, dtype=jnp.int32)[None, :]).astype(jnp.int32)
    rank = jnp.cumsum(onehot, axis=0) - onehot
    within = jnp.sum(rank * onehot, axis=1)
    slot_ids = (flat * capacity + within).reshape(tokens, topk)
    places = jnp.arange(experts * capacity, dtype=jnp.int32)
    hits = (slot_ids[:, :, None] == places[None, None, :]).astype(jnp.float32)
    normed = scores / jnp.sum(scores, axis=1, keepdims=True)
    member = jnp.sum(hits, axis=1)
    weighted = jnp.sum(hits * normed[:, :, None], axis=1)
    return (member, weighted)


def pick_rows(member, rows):
    slots = jnp.einsum(
        "te,td->ed", member.astype(jnp.bfloat16), rows, preferred_element_type=jnp.float32
    )
    return slots.astype(jnp.bfloat16)


def expert_forward(rows3, w_gate, w_up, w_down):
    width = rows3.shape[-1]
    flat = rows3.reshape(-1, width)
    first = jnp.dot(flat, w_gate, preferred_element_type=jnp.float32)
    second = jnp.dot(flat, w_up, preferred_element_type=jnp.float32)
    hidden = (jax.nn.silu(first) * second).astype(jnp.bfloat16)
    parts = jnp.dot(hidden, w_down, preferred_element_type=jnp.float32).astype(jnp.bfloat16)
    return parts.reshape(rows3.shape)


def expert_backward(rows3, grads3, w_gate, w_up, w_down):
    width = rows3.shape[-1]
    flat = rows3.reshape(-1, width)
    first = jnp.dot(flat, w_gate, preferred_element_type=jnp.float32)
    second = jnp.dot(flat, w_up, preferred_element_type=jnp.float32)
    d_hidden = lax.dot_general(
        grads3.reshape(-1, width),
        w_down,
        (((1,), (1,)), ((), ())),
        preferred_element_type=jnp.float32,
    )
    sigm = 1.0 / (1.0 + jnp.exp(-first))
    d_first = (d_hidden * second * sigm * (1.0 + first * (1.0 - sigm))).astype(jnp.bfloat16)
    d_second = (d_hidden * first * sigm).astype(jnp.bfloat16)
    back = lax.dot_general(
        d_first, w_gate, (((1,), (1,)), ((), ())), preferred_element_type=jnp.float32
    )
    back = back + lax.dot_general(
        d_second, w_up, (((1,), (1,)), ((), ())), preferred_element_type=jnp.float32
    )
    return back.astype(jnp.bfloat16).reshape(rows3.shape)


def expert_work(arrived, weights):
    w_gate, w_up, w_down = weights
    kinds = arrived.shape[0]
    if kinds == 1:
        return expert_forward(arrived[0], w_gate, w_up, w_down)[None]
    return expert_backward(arrived[0], arrived[1], w_gate, w_up, w_down)[None]


def pass_rows(payload, weights):
    kinds, experts, capacity, width = payload.shape
    spread = jnp.broadcast_to(payload[:, :, None], (kinds, experts, GROUP, capacity, width))
    spread = spread.reshape(kinds, experts * GROUP, capacity, width)
    returned = lax.all_to_all(
        expert_work(
            lax.all_to_all(spread, "expert", split_axis=1, concat_axis=1, tiled=True), weights
        ),
        "expert",
        split_axis=1,
        concat_axis=1,
        tiled=True,
    )
    outkinds = returned.shape[0]
    summed = jnp.sum(
        returned.reshape(outkinds, experts, GROUP, capacity, width).astype(jnp.float32), axis=2
    )
    return summed.reshape(outkinds, experts * capacity, width)


def body(
    fwd_tokens,
    fwd_routes,
    fwd_scores,
    bwd_tokens,
    bwd_routes,
    bwd_scores,
    out_grad,
    gate_weight,
    up_weight,
    down_weight,
):
    experts = lax.axis_size("expert") // GROUP
    tokens = fwd_tokens.shape[1]
    topk = fwd_routes.shape[2]
    width = fwd_tokens.shape[2]
    capacity = min(tokens, max(6, (tokens * topk + experts - 1) // experts + 2))
    weights = (gate_weight[0], up_weight[0], down_weight[0])
    member_f, weight_f = route_tables(fwd_routes[0], fwd_scores[0], capacity, experts)
    member_b, weight_b = route_tables(bwd_routes[0], bwd_scores[0], capacity, experts)
    send_f = pick_rows(member_f, fwd_tokens[0]).reshape(experts, capacity, width)
    send_x = pick_rows(member_b, bwd_tokens[0]).reshape(experts, capacity, width)
    route_grad = jnp.einsum(
        "te,td->ed", weight_b, out_grad[0].astype(jnp.float32), precision=lax.Precision.HIGHEST
    )
    send_g = route_grad.astype(jnp.bfloat16).reshape(experts, capacity, width)
    sum_f = pass_rows(send_f[None], weights)[0]
    sum_b = pass_rows(jnp.stack((send_x, send_g)), weights)[0]
    layer_out = jnp.dot(weight_f, sum_f, precision=lax.Precision.HIGHEST).astype(jnp.bfloat16)[None]
    input_grad = jnp.dot(member_b, sum_b, precision=lax.Precision.HIGHEST).astype(jnp.bfloat16)[
        None
    ]
    next_input = from_behind(layer_out, "pipe", 1)
    prev_grad = from_behind(input_grad, "pipe", -1)
    return (next_input, prev_grad)


def solution(mesh):
    placed = (
        P("pipe", "expert", None),
        P("pipe", "expert", None),
        P("pipe", "expert", None),
        P("pipe", "expert", None),
        P("pipe", "expert", None),
        P("pipe", "expert", None),
        P("pipe", "expert", None),
        P("pipe", None, "expert"),
        P("pipe", None, "expert"),
        P("pipe", "expert", None),
    )
    return jax.shard_map(
        body,
        mesh=mesh,
        in_specs=placed,
        out_specs=(P("pipe", "expert", None), P("pipe", "expert", None)),
        check_vma=False,
    )
```

profile of v0, /device:TPU:30, one launch (start us, length us, event | category | flops | bytes accessed | tf_op | source)
XLA Modules:
  0.0 810.3 jit_solution(13249150855847399699)
XLA Ops:
  0.6 0.0 copy-start
  0.6 0.8 copy.39
  1.5 0.1 eq.56
  1.6 0.1 fusion.36
  1.6 0.1 reduce_window_sum.17
  1.7 0.2 select_reduce_fusion.3
  1.9 0.1 reduce_sum.95
  2.0 0.1 copy.40
  2.1 0.7 bitcast_add_fusion.1
  2.8 0.7 reduce_sum.96
  3.5 0.7 bitcast_divide_fusion.1
  4.1 0.1 convert_reduce_fusion.3
  4.2 1.2 convolution_convert_fusion.3
  5.4 0.1 broadcast_in_dim.12
  5.5 2.1 broadcast_in_dim.13
  7.6 19.0 %all-to-all-start = ((bf16[1,64,6,3584]{3,2,0,1:T(8,128)(2,1)}), bf16[1,64,6,3584]{3,2,0,1:T(8,128)(2,1)}, u32[]{:S(2)}, u32[]{:S(2)}) async-start(bf16[1,64,6,3584]{3,2,0,1:T(8,128)(2,1)} %bitcast.66), calls=%async_computation | async-start | bytes 7340032 | tf_op jit(solution)/shard_map/all_to_all | solution.py:84
  26.7 0.1 copy.42
  26.7 0.1 eq.63
  26.8 0.1 fusion.35
  26.9 0.1 reduce_window_sum.18
  27.0 0.2 select_reduce_fusion.1
  27.1 0.1 reduce_sum.101
  27.2 0.1 copy.43
  27.4 0.1 select_reduce_fusion
  27.5 0.0 copy-done.4
  27.5 0.3 convolution_convert_fusion.2
  27.7 0.1 stack_reshape.6
  27.9 0.5 convolution_convert_fusion.1
  28.4 0.1 stack_reshape.7
  28.5 0.2 pad_maximum_fusion
  28.7 0.7 copy.44
  29.4 161.7 %all-to-all-done = bf16[1,64,6,3584]{3,2,0,1:T(8,128)(2,1)} async-done(((bf16[1,64,6,3584]{3,2,0,1:T(8,128)(2,1)}), bf16[1,64,6,3584]{3,2,0,1:T(8,128)(2,1)}, u32[]{:S(2)}, u32[]{:S(2)}) %all-to-all-start) | async-done | bytes 2752544 | tf_op jit(solution)/shard_map/all_to_all | solution.py:84
  191.1 5.2 broadcast_in_dim.16
  196.3 9.4 %all-to-all-start.2 = ((bf16[2,64,6,3584]{3,0,2,1:T(2,128)(2,1)}), bf16[2,64,6,3584]{3,0,2,1:T(2,128)(2,1)}, u32[]{:S(2)}, u32[]{:S(2)}) async-start(bf16[2,64,6,3584]{3,0,2,1:T(2,128)(2,1)} %bitcast.63), calls=%async_computation.2 | async-start | bytes 11010048 | tf_op jit(solution)/shard_map/all_to_all | solution.py:84
  205.8 0.0 copy-start.2
  205.8 5.6 reshape_squeeze.11
  211.3 2.7 fusion.19
  214.1 6.3 convolution_convert_fusion
  220.4 5.4 broadcast_in_dim_reshape.8
  225.8 224.4 %all-to-all-done.2 = bf16[2,64,6,3584]{3,0,2,1:T(2,128)(2,1)} async-done(((bf16[2,64,6,3584]{3,0,2,1:T(2,128)(2,1)}), bf16[2,64,6,3584]{3,0,2,1:T(2,128)(2,1)}, u32[]{:S(2)}, u32[]{:S(2)}) %all-to-all-start.2) | async-done | bytes 5505056 | tf_op jit(solution)/shard_map/all_to_all | solution.py:84
  450.2 8.1 all-to-all-start.1
  458.4 37.1 %slice_reduce_fusion = (bf16[64,6,3584]{2,1,0:T(8,128)(2,1)}, bf16[64,6,3584]{2,1,0:T(8,128)(2,1)}) fusion(bf16[2,64,6,3584]{3,0,2,1:T(2,128)(2,1)} %all-to-all-done.2), kind=kLoop, calls=%fused_computation.5 | loop fusion | bytes 11010048 | tf_op jit(solution)/shard_map/slice | solution.py:75
  495.4 5.5 reshape_squeeze.13
  500.9 5.4 reshape_squeeze.12
  506.4 2.8 fusion.17
  509.2 0.9 fusion.8
  510.1 7.3 fusion.7
  517.3 5.0 fusion
  522.3 5.5 broadcast_in_dim_reshape.9
  527.8 95.1 %all-to-all-done.1 = bf16[1,64,6,3584]{3,2,0,1:T(8,128)(2,1)} async-done(((bf16[1,64,6,3584]{3,2,0,1:T(8,128)(2,1)}), bf16[1,64,6,3584]{3,2,0,1:T(8,128)(2,1)}, u32[]{:S(2)}, u32[]{:S(2)}) %all-to-all-start.1) | async-done | bytes 2752544 | tf_op jit(solution)/shard_map/all_to_all | solution.py:82
  622.8 9.4 %all-to-all-start.3 = ((bf16[1,64,6,3584]{3,2,0,1:T(8,128)(2,1)}), bf16[1,64,6,3584]{3,2,0,1:T(8,128)(2,1)}, u32[]{:S(2)}, u32[]{:S(2)}) async-start(bf16[1,64,6,3584]{3,2,0,1:T(8,128)(2,1)} %bitcast.65), calls=%async_computation.3 | async-start | bytes 7340032 | tf_op jit(solution)/shard_map/all_to_all | solution.py:82
  632.3 2.9 convert_reduce_fusion.1
  635.2 0.1 squeeze_reshape.6
  635.3 0.4 fusion.1
  635.7 2.4 collective-permute-start
  638.1 158.7 %all-to-all-done.3 = bf16[1,64,6,3584]{3,2,0,1:T(8,128)(2,1)} async-done(((bf16[1,64,6,3584]{3,2,0,1:T(8,128)(2,1)}), bf16[1,64,6,3584]{3,2,0,1:T(8,128)(2,1)}, u32[]{:S(2)}, u32[]{:S(2)}) %all-to-all-start.3) | async-done | bytes 2752544 | tf_op jit(solution)/shard_map/all_to_all | solution.py:82
  796.8 2.9 convert_reduce_fusion
  799.6 0.1 squeeze_reshape.7
  799.7 0.4 fusion.2
  800.2 2.7 collective-permute-start.1
  802.9 0.0 collective-permute-done
  803.0 6.0 collective-permute-done.1
  809.0 0.6 copy.50
  809.6 0.6 copy.51
  (16 shorter events, 0.1 us)
Async XLA Ops:
  0.6 213.5 %copy-start = (bf16[1,3584,128]{2,1,0:T(8,128)(2,1)S(1)}, bf16[1,3584,128]{2,1,0:T(8,128)(2,1)}, u32[]{:S(2)}) copy-start(bf16[1,3584,128]{2,1,0:T(8,128)(2,1)} %param.18) | copy-start | bytes 2752516
  7.6 19.0 %copy-start.6 = (s32[1,16,2]{1,2,0:T(2,128)S(1)}, s32[1,16,2]{1,2,0:T(2,128)}, u32[]{:S(2)}) copy-start(s32[1,16,2]{1,2,0:T(2,128)} %param.14) | copy-start | bytes 388
  7.6 19.7 %copy-start.7 = (f32[1,16,2]{1,2,0:T(2,128)S(1)}, f32[1,16,2]{1,2,0:T(2,128)}, u32[]{:S(2)}) copy-start(f32[1,16,2]{1,2,0:T(2,128)} %param.15) | copy-start | bytes 388
  7.6 19.8 %copy-start.4 = (bf16[1,16,3584]{2,1,0:T(8,128)(2,1)S(1)}, bf16[1,16,3584]{2,1,0:T(8,128)(2,1)}, u32[]{:S(2)}) copy-start(bf16[1,16,3584]{2,1,0:T(8,128)(2,1)} %param.13) | copy-start | bytes 344068
  7.6 20.3 %copy-start.5 = (bf16[1,16,3584]{2,1,0:T(8,128)(2,1)S(1)}, bf16[1,16,3584]{2,1,0:T(8,128)(2,1)}, u32[]{:S(2)}) copy-start(bf16[1,16,3584]{2,1,0:T(8,128)(2,1)} %param.16) | copy-start | bytes 344068
  7.6 183.5 %all-to-all-start = ((bf16[1,64,6,3584]{3,2,0,1:T(8,128)(2,1)}), bf16[1,64,6,3584]{3,2,0,1:T(8,128)(2,1)}, u32[]{:S(2)}, u32[]{:S(2)}) async-start(bf16[1,64,6,3584]{3,2,0,1:T(8,128)(2,1)} %bitcast.66), calls=%async_computation | async-start | bytes 7340032 | tf_op jit(solution)/shard_map/all_to_all | solution.py:84
  196.3 253.9 %all-to-all-start.2 = ((bf16[2,64,6,3584]{3,0,2,1:T(2,128)(2,1)}), bf16[2,64,6,3584]{3,0,2,1:T(2,128)(2,1)}, u32[]{:S(2)}, u32[]{:S(2)}) async-start(bf16[2,64,6,3584]{3,0,2,1:T(2,128)(2,1)} %bitcast.63), calls=%async_computation.2 | async-start | bytes 11010048 | tf_op jit(solution)/shard_map/all_to_all | solution.py:84
  205.8 5.6 copy-start.2
  211.3 2.7 copy-start.3
  450.2 172.6 %all-to-all-start.1 = ((bf16[1,64,6,3584]{3,2,0,1:T(8,128)(2,1)}), bf16[1,64,6,3584]{3,2,0,1:T(8,128)(2,1)}, u32[]{:S(2)}, u32[]{:S(2)}) async-start(bf16[1,64,6,3584]{3,2,0,1:T(8,128)(2,1)} %bitcast.64), calls=%async_computation.1 | async-start | bytes 7340032 | tf_op jit(solution)/shard_map/all_to_all | solution.py:82
  506.4 2.8 copy-start.1
  622.8 173.9 %all-to-all-start.3 = ((bf16[1,64,6,3584]{3,2,0,1:T(8,128)(2,1)}), bf16[1,64,6,3584]{3,2,0,1:T(8,128)(2,1)}, u32[]{:S(2)}, u32[]{:S(2)}) async-start(bf16[1,64,6,3584]{3,2,0,1:T(8,128)(2,1)} %bitcast.65), calls=%async_computation.3 | async-start | bytes 7340032 | tf_op jit(solution)/shard_map/all_to_all | solution.py:82
  635.7 167.2 %collective-permute-start = (bf16[1,16,3584]{2,1,0:T(8,128)(2,1)S(1)}, bf16[1,16,3584]{2,1,0:T(8,128)(2,1)S(1)}, u32[]{:S(2)}, u32[]{:S(2)}) collective-permute-start(bf16[1,16,3584]{2,1,0:T(8,128)(2,1)S(1)} %fusion.1), channel_id=1, source_target_pairs={{0,64},{64,128},{128,192},{192,256},{256,320},{320,384},{384,448},... | collective-permute-start | bytes 344072 | tf_op jit(solution)/shard_map/ppermute | solution.py:12
  800.2 8.8 %collective-permute-start.1 = (bf16[1,16,3584]{2,1,0:T(8,128)(2,1)S(1)}, bf16[1,16,3584]{2,1,0:T(8,128)(2,1)S(1)}, u32[]{:S(2)}, u32[]{:S(2)}) collective-permute-start(bf16[1,16,3584]{2,1,0:T(8,128)(2,1)S(1)} %fusion.2), channel_id=1, source_target_pairs={{0,448},{64,0},{128,64},{192,128},{256,192},{320,256},{384,320},{4... | collective-permute-start | bytes 344072 | tf_op jit(solution)/shard_map/ppermute | solution.py:12
where the time goes:
time: 812 us; the launch traced here: 810 us
  waiting for transfers between devices  646 us (80%)
  local copies, waits for them, and re-layouts  75.8 us (9%)
  starting transfers between devices  51.2 us (6%)
  matrix products  27.7 us (3%)
  other arithmetic  8.81 us (1%)
    all_to_all x2, waiting for transfers between devices, pass_rows(): lax.all_to_all(spread, 'expert', split_axis=1, concat_axis=1, tiled=True)  386 us
    all_to_all x2, waiting for transfers between devices, pass_rows(): lax.all_to_all(expert_work(lax.all_to_all(spread, 'expert', split_axis=1,...  254 us
    slice x1, local copies, waits for them, and re-layouts, expert_work(): return expert_backward(arrived[0], arrived[1], w_gate, w_up, w_down)[None]  37.1 us
    all_to_all x2, starting transfers between devices, pass_rows(): lax.all_to_all(spread, 'expert', split_axis=1, concat_axis=1, tiled=True)  28.5 us
    all_to_all x2, starting transfers between devices, pass_rows(): lax.all_to_all(expert_work(lax.all_to_all(spread, 'expert', split_axis=1,...  17.5 us
  transfers between devices with their start and end apart: 6, of which 5 were waited for; matrix products, arithmetic and copies ran while one was open for 12% of the time, Pallas kernels for 0%

commit v1 on v0

v1 whole, which is shorter than its diff:
```python
import jax
import jax.numpy as jnp
from jax import lax
from jax.sharding import Mesh
from jax.sharding import PartitionSpec as P

GROUP = 8


def from_behind(value, axis, steps):
    count = lax.axis_size(axis)
    pairs = [(source, (source + steps) % count) for source in range(count)]
    return lax.ppermute(value, axis, pairs)


def route_tables(routes, scores, capacity, experts):
    tokens, topk = routes.shape
    flat = routes.reshape(-1)
    onehot = (flat[:, None] == jnp.arange(experts, dtype=jnp.int32)[None, :]).astype(jnp.int32)
    rank = jnp.cumsum(onehot, axis=0) - onehot
    within = jnp.sum(rank * onehot, axis=1)
    slot_ids = (flat * capacity + within).reshape(tokens, topk)
    places = jnp.arange(experts * capacity, dtype=jnp.int32)
    hits = (slot_ids[:, :, None] == places[None, None, :]).astype(jnp.float32)
    normed = scores / jnp.sum(scores, axis=1, keepdims=True)
    member = jnp.sum(hits, axis=1)
    weighted = jnp.sum(hits * normed[:, :, None], axis=1)
    return (member, weighted)


def pick_rows(member, rows):
    slots = jnp.einsum(
        "te,td->ed", member.astype(jnp.bfloat16), rows, preferred_element_type=jnp.float32
    )
    return slots.astype(jnp.bfloat16)


def expert_forward(flat, w_gate, w_up, w_down):
    first = jnp.dot(flat, w_gate, preferred_element_type=jnp.float32)
    second = jnp.dot(flat, w_up, preferred_element_type=jnp.float32)
    hidden = (jax.nn.silu(first) * second).astype(jnp.bfloat16)
    return jnp.dot(hidden, w_down, preferred_element_type=jnp.float32).astype(jnp.bfloat16)


def expert_backward(flat, grads, w_gate, w_up, w_down):
    first = jnp.dot(flat, w_gate, preferred_element_type=jnp.float32)
    second = jnp.dot(flat, w_up, preferred_element_type=jnp.float32)
    d_hidden = lax.dot_general(
        grads, w_down, (((1,), (1,)), ((), ())), preferred_element_type=jnp.float32
    )
    sigm = 1.0 / (1.0 + jnp.exp(-first))
    d_first = (d_hidden * second * sigm * (1.0 + first * (1.0 - sigm))).astype(jnp.bfloat16)
    d_second = (d_hidden * first * sigm).astype(jnp.bfloat16)
    back = lax.dot_general(
        d_first, w_gate, (((1,), (1,)), ((), ())), preferred_element_type=jnp.float32
    )
    back = back + lax.dot_general(
        d_second, w_up, (((1,), (1,)), ((), ())), preferred_element_type=jnp.float32
    )
    return back.astype(jnp.bfloat16)


def body(
    fwd_tokens,
    fwd_routes,
    fwd_scores,
    bwd_tokens,
    bwd_routes,
    bwd_scores,
    out_grad,
    gate_weight,
    up_weight,
    down_weight,
):
    experts = lax.axis_size("eg")
    tokens = fwd_tokens.shape[1]
    topk = fwd_routes.shape[2]
    width = fwd_tokens.shape[2]
    capacity = min(tokens, max(6, (tokens * topk + experts - 1) // experts + 2))
    w_gate, w_up, w_down = gate_weight[0], up_weight[0], down_weight[0]
    member_f, weight_f = route_tables(fwd_routes[0], fwd_scores[0], capacity, experts)
    member_b, weight_b = route_tables(bwd_routes[0], bwd_scores[0], capacity, experts)
    send_f = pick_rows(member_f, fwd_tokens[0])
    send_x = pick_rows(member_b, bwd_tokens[0])
    route_grad = jnp.einsum(
        "te,td->ed", weight_b, out_grad[0].astype(jnp.float32), precision=lax.Precision.HIGHEST
    )
    send_g = route_grad.astype(jnp.bfloat16)
    payload = jnp.stack((send_f, send_x, send_g)).reshape(3, experts, capacity, width)
    crossed = lax.all_to_all(payload, "eg", split_axis=1, concat_axis=1, tiled=True)
    arrived = lax.all_gather(crossed, "ei", axis=1, tiled=False)
    rows = arrived.reshape(3, -1, width)
    out_f = expert_forward(rows[0], w_gate, w_up, w_down)
    out_b = expert_backward(rows[1], rows[2], w_gate, w_up, w_down)
    parts = jnp.stack((out_f, out_b)).reshape((2,) + arrived.shape[1:])
    summed = lax.psum_scatter(parts, "ei", scatter_dimension=1, tiled=True)
    summed = summed.reshape(2, experts, capacity, width)
    home = lax.all_to_all(summed, "eg", split_axis=1, concat_axis=1, tiled=True)
    home = home.reshape(2, experts * capacity, width).astype(jnp.float32)
    layer_out = jnp.dot(weight_f, home[0], precision=lax.Precision.HIGHEST).astype(jnp.bfloat16)[
        None
    ]
    input_grad = jnp.dot(member_b, home[1], precision=lax.Precision.HIGHEST).astype(jnp.bfloat16)[
        None
    ]
    next_input = from_behind(layer_out, "pipe", 1)
    prev_grad = from_behind(input_grad, "pipe", -1)
    return (next_input, prev_grad)


def solution(mesh):
    pipe, expert = mesh.devices.shape
    split = Mesh(mesh.devices.reshape(pipe, expert // GROUP, GROUP), ("pipe", "eg", "ei"))
    rows = P("pipe", ("eg", "ei"), None)
    cols = P("pipe", None, ("eg", "ei"))
    placed = (rows, rows, rows, rows, rows, rows, rows, cols, cols, rows)
    return jax.shard_map(
        body,
        mesh=split,
        in_specs=placed,
        out_specs=(rows, rows),
        check_vma=False,
    )
```

time: 812 us -> 428 us (0.53)
  the two profiles are of different devices: /device:TPU:30 before, /device:TPU:64 now
where the time goes in v1:
time: 428 us; the launch traced here: 427 us
  waiting for transfers between devices  164 us (38%)
  blocking collectives  142 us (33%)
  local copies, waits for them, and re-layouts  58.9 us (14%)
  matrix products  30 us (7%)
  between operations  14.2 us (3%)
  other arithmetic  10.4 us (2%)
  starting transfers between devices  6.64 us (2%)
    all_to_all x1, blocking collectives, body(): lax.all_to_all(payload, 'eg', split_axis=1, concat_axis=1, tiled=True)  87.1 us
    all_gather x1, waiting for transfers between devices, body(): arrived = lax.all_gather(crossed, 'ei', axis=1, tiled=False)  86.1 us
    reduce_scatter x1, waiting for transfers between devices, body(): summed = lax.psum_scatter(parts, 'ei', scatter_dimension=1, tiled=True)  71.5 us
    all_to_all x1, blocking collectives, body(): home = lax.all_to_all(summed, 'eg', split_axis=1, concat_axis=1, tiled=True)  54.8 us
    another operation x3, local copies, waits for them, and re-layouts, body(): parts = jnp.stack((out_f, out_b)).reshape((2,) + arrived.shape[1:])  15.2 us
    squeeze x2, local copies, waits for them, and re-layouts, body(): out_b = expert_backward(rows[1], rows[2], w_gate, w_up, w_down)  11 us
    slice x2, local copies, waits for them, and re-layouts, body(): out_f = expert_forward(rows[0], w_gate, w_up, w_down)  8.58 us
  transfers between devices with their start and end apart: 4, of which 4 were waited for; matrix products, arithmetic and copies ran while one was open for 0% of the time, Pallas kernels for 0%

profile of v1, /device:TPU:64, one launch (start us, length us, event | category | flops | bytes accessed | tf_op | source)
XLA Modules:
  0.0 426.5 jit_solution(2733729603735968163)
XLA Ops:
  7.2 0.8 reduce_sum.78
  8.0 0.7 bitcast_divide_fusion.1
  8.7 0.7 reduce_sum.84
  9.4 0.7 bitcast_divide_fusion
  10.1 0.8 copy.54
  10.8 0.1 eq.56
  10.9 0.8 copy.56
  11.7 0.1 eq.63
  11.8 0.1 fusion.35
  11.8 0.1 reduce_window_sum.18
  11.9 0.2 select_reduce_fusion.1
  12.1 0.1 reduce_sum.82
  12.2 0.1 copy.57
  12.3 0.7 bitcast_add_fusion
  13.0 0.1 fusion.36
  13.0 0.1 reduce_window_sum.17
  13.1 0.2 select_reduce_fusion.3
  13.3 0.1 reduce_sum.77
  13.4 0.1 copy.55
  13.4 0.7 bitcast_add_fusion.1
  14.1 0.1 convert_reduce_fusion
  14.2 1.4 convolution_convert_fusion.1
  15.6 0.1 stack.23
  15.7 0.1 convert_reduce_fusion.1
  15.8 1.2 convolution_convert_fusion.3
  17.0 0.1 stack.21
  17.1 0.3 convolution_convert_fusion.2
  17.4 0.1 stack.22
  17.5 0.3 pad_maximum_fusion.1
  17.9 0.1 copy.58
  18.0 87.1 %all_to_all.10 = bf16[3,8,6,3584]{3,2,0,1:T(8,128)(2,1)S(1)} all-to-all(bf16[3,8,6,3584]{3,2,0,1:T(8,128)(2,1)S(1)} %copy.58), channel_id=1, replica_groups=mesh['pipe'=8,'eg'=8,'ei'=8] {'eg'}, dimensions={1} | all-to-all | bytes 2064384 | tf_op jit(solution)/shard_map/all_to_all | solution.py:90
  105.1 1.3 copy.59
  106.5 86.1 %all-gather.3.cloned.1.call-done = bf16[3,64,6,3584]{3,1,2,0:T(8,128)(2,1)} async-done(((bf16[3,8,6,3584]{3,1,2,0:T(8,128)(2,1)}), bf16[3,64,6,3584]{3,1,2,0:T(8,128)(2,1)}) %all-gather.3.cloned.1.call-update) | async-done | bytes 8257552 | tf_op jit(solution)/shard_map/all_gather | solution.py:91
  192.6 5.3 %fusion.42 = (bf16[1,64,6,3584]{3,1,2,0:T(8,128)(2,1)S(1)}, bf16[1,64,6,3584]{3,1,2,0:T(8,128)(2,1)}, bf16[1,64,6,3584]{3,1,2,0:T(8,128)(2,1)}) fusion(bf16[3,64,6,3584]{3,1,2,0:T(8,128)(2,1)} %all-gather.3.cloned.1.call-done), kind=kLoop, calls=%fused_computation.69 | loop fusion | bytes 16515072 | tf_op jit(solution)/shard_map/slice | solution.py:93
  197.8 3.3 copy.60
  201.2 5.6 %squeeze.44 = bf16[384,3584]{1,0:T(8,128)(2,1)} reshape(bf16[1,64,6,3584]{3,2,1,0:T(8,128)(2,1)} %copy.60) | data formatting | bytes 5505024 | tf_op jit(solution)/shard_map/squeeze | solution.py:93
  206.7 2.7 fusion.19
  209.5 6.4 %convolution_convert_fusion = bf16[384,3584]{1,0:T(8,128)(2,1)} fusion(bf16[384,3584]{1,0:T(8,128)(2,1)} %squeeze.44, bf16[1,128,3584]{2,1,0:T(8,128)(2,1)S(1)} %copy-done.3, bf16[1,3584,128]{2,1,0:T(8,128)(2,1)S(1)} %copy-done, f32[384,128]{1,0:T(8,128)S(1)} %fusion.19), kind=kOutput, calls=%fused_computation.3 | convolution fusion | flops 706314240 | bytes 7536640 | tf_op jit(solution)/shard_map/dot_general | solution.py:42
  215.8 5.4 %stack.25 = bf16[1,8,8,6,3584]{4,3,2,1,0:T(8,128)(2,1)} reshape(bf16[384,3584]{1,0:T(8,128)(2,1)} %convolution_convert_fusion) | data formatting | bytes 5505024 | tf_op jit(solution)/shard_map/stack | solution.py:95
  221.2 5.1 %copy.61 = bf16[1,64,6,3584]{3,2,1,0:T(8,128)(2,1)} copy(bf16[1,64,6,3584]{3,1,2,0:T(8,128)(2,1)} %get-tuple-element.9) | data formatting | bytes 5505024 | tf_op jit(solution)/shard_map/slice | solution.py:94
  226.4 5.5 %squeeze.48 = bf16[384,3584]{1,0:T(8,128)(2,1)} reshape(bf16[1,64,6,3584]{3,2,1,0:T(8,128)(2,1)} %copy.61) | data formatting | bytes 5505024 | tf_op jit(solution)/shard_map/squeeze | solution.py:94
  231.9 2.8 fusion.8
  234.7 3.3 copy.62
  238.0 5.5 %squeeze.49 = bf16[384,3584]{1,0:T(8,128)(2,1)} reshape(bf16[1,64,6,3584]{3,2,1,0:T(8,128)(2,1)} %copy.62) | data formatting | bytes 5505024 | tf_op jit(solution)/shard_map/squeeze | solution.py:94
  243.5 2.6 fusion.17
  246.1 7.2 %fusion.7 = f32[384,3584]{1,0:T(8,128)} fusion(f32[384,128]{1,0:T(8,128)S(1)} %fusion.8, bf16[384,3584]{1,0:T(8,128)(2,1)} %squeeze.49, bf16[1,3584,128]{2,1,0:T(8,128)(2,1)S(1)} %copy-done, bf16[1,3584,128]{2,1,0:T(8,128)(2,1)S(1)} %copy-done.2, f32[384,128]{1,0:T(8,128)S(1)} %fusion.17), kind=kOutput, calls=%fused_computation.18 | convolution fusion | flops 705134592 | bytes 10485760 | tf_op jit(solution)/shard_map/dot_general | solution.py:54
  253.3 5.0 %fusion = bf16[384,3584]{1,0:T(8,128)(2,1)} fusion(f32[384,3584]{1,0:T(8,128)} %fusion.7, bf16[1,3584,128]{2,1,0:T(8,128)(2,1)S(1)} %copy-done, f32[384,128]{1,0:T(8,128)S(1)} %fusion.8, f32[384,128]{1,0:T(8,128)S(1)} %fusion.17), kind=kOutput, calls=%fused_computation.2 | convolution fusion | flops 355368960 | bytes 9568256 | tf_op jit(solution)/shard_map/dot_general | solution.py:57
  258.3 5.4 %stack.26 = bf16[1,8,8,6,3584]{4,3,2,1,0:T(8,128)(2,1)} reshape(bf16[384,3584]{1,0:T(8,128)(2,1)} %fusion) | data formatting | bytes 5505024 | tf_op jit(solution)/shard_map/stack | solution.py:95
  263.7 5.1 %pad_maximum_fusion = bf16[2,8,8,6,3584]{4,3,2,1,0:T(8,128)(2,1)S(1)} fusion(bf16[1,8,8,6,3584]{4,3,2,1,0:T(8,128)(2,1)} %stack.26, bf16[1,8,8,6,3584]{4,3,2,1,0:T(8,128)(2,1)} %stack.25), kind=kLoop, calls=%fused_computation | loop fusion | flops 2752512 | bytes 11010048 | tf_op jit(solution)/shard_map/stack | solution.py:95
  268.8 4.4 %copy.63 = bf16[2,8,8,6,3584]{4,2,3,0,1:T(8,128)(2,1)} copy(bf16[2,8,8,6,3584]{4,3,2,1,0:T(8,128)(2,1)S(1)} %pad_maximum_fusion) | data formatting | bytes 11010048 | tf_op jit(solution)/shard_map/stack | solution.py:95
  273.2 71.5 %reduce-scatter.2.cloned.1.call-done = bf16[2,1,8,6,3584]{4,2,3,0,1:T(8,128)(2,1)} async-done(((bf16[2,8,8,6,3584]{4,2,3,0,1:T(8,128)(2,1)}), bf16[2,1,8,6,3584]{4,2,3,0,1:T(8,128)(2,1)}) %reduce-scatter.2.cloned.1.call-update) | async-done | bytes 688144 | tf_op jit(solution)/shard_map/reduce_scatter | solution.py:96
  344.7 1.8 copy.64
  346.5 54.8 %all_to_all.11 = bf16[2,8,6,3584]{3,0,2,1:T(2,128)(2,1)S(1)} all-to-all(bf16[2,8,6,3584]{3,0,2,1:T(2,128)(2,1)S(1)} %copy.64), channel_id=1, replica_groups=mesh['pipe'=8,'eg'=8,'ei'=8] {'eg'}, dimensions={1} | all-to-all | bytes 1376256 | tf_op jit(solution)/shard_map/all_to_all | solution.py:98
  401.2 2.9 slice_reduce_fusion
  404.2 0.1 squeeze.51
  404.3 0.3 fusion.2
  404.5 4.6 %collective-permute-start.1 = (bf16[1,16,3584]{2,1,0:T(8,128)(2,1)S(1)}, bf16[1,16,3584]{2,1,0:T(8,128)(2,1)S(1)}, u32[]{:S(2)}, u32[]{:S(2)}) collective-permute-start(bf16[1,16,3584]{2,1,0:T(8,128)(2,1)S(1)} %fusion.2), channel_id=1, source_target_pairs={{0,448},{64,0},{128,64},{192,128},{256,192},{320,256},{384,320},{4... | collective-permute-start | bytes 344072 | tf_op jit(solution)/shard_map/ppermute | solution.py:13
  409.2 0.1 squeeze.50
  409.3 0.3 fusion.1
  409.6 1.9 collective-permute-start
  411.5 0.8 collective-permute-done.1
  412.3 6.0 %collective-permute-done = bf16[1,16,3584]{2,1,0:T(8,128)(2,1)S(1)} collective-permute-done((bf16[1,16,3584]{2,1,0:T(8,128)(2,1)S(1)}, bf16[1,16,3584]{2,1,0:T(8,128)(2,1)S(1)}, u32[]{:S(2)}, u32[]{:S(2)}) %collective-permute-start) | collective-permute-done | bytes 114720 | tf_op jit(solution)/shard_map/ppermute | solution.py:13
  418.4 0.6 copy.69
  419.0 0.6 copy.70
  (14 shorter events, 0.1 us)
Async XLA Ops:
  7.2 202.3 %copy-start = (bf16[1,3584,128]{2,1,0:T(8,128)(2,1)S(1)}, bf16[1,3584,128]{2,1,0:T(8,128)(2,1)}, u32[]{:S(2)}) copy-start(bf16[1,3584,128]{2,1,0:T(8,128)(2,1)} %param.18) | copy-start | bytes 2752516
  7.2 9.9 %copy-start.4 = (bf16[1,16,3584]{2,1,0:T(8,128)(2,1)S(1)}, bf16[1,16,3584]{2,1,0:T(8,128)(2,1)}, u32[]{:S(2)}) copy-start(bf16[1,16,3584]{2,1,0:T(8,128)(2,1)} %param.13) | copy-start | bytes 344068
  7.2 185.4 %all-gather.3.cloned.1.call-start = ((), (), s32[]{:S(2)}) async-start(), calls=%async_computation.4 | async-start | bytes 9289728 | tf_op jit(solution)/shard_map/all_gather | solution.py:91
  106.5 238.2 %reduce-scatter.2.cloned.1.call-start = ((), (), s32[]{:S(2)}) async-start(), calls=%async_computation.3 | async-start | bytes 6193152 | tf_op jit(solution)/shard_map/reduce_scatter | solution.py:96
  201.2 5.6 %copy-start.2 = (bf16[1,3584,128]{2,1,0:T(8,128)(2,1)S(1)}, bf16[1,3584,128]{2,1,0:T(8,128)(2,1)}, u32[]{:S(2)}) copy-start(bf16[1,3584,128]{2,1,0:T(8,128)(2,1)} %param.17) | copy-start | bytes 2752516
  206.7 2.7 copy-start.3
  231.9 2.8 copy-start.1
  404.5 7.8 %collective-permute-start.1 = (bf16[1,16,3584]{2,1,0:T(8,128)(2,1)S(1)}, bf16[1,16,3584]{2,1,0:T(8,128)(2,1)S(1)}, u32[]{:S(2)}, u32[]{:S(2)}) collective-permute-start(bf16[1,16,3584]{2,1,0:T(8,128)(2,1)S(1)} %fusion.2), channel_id=1, source_target_pairs={{0,448},{64,0},{128,64},{192,128},{256,192},{320,256},{384,320},{4... | collective-permute-start | bytes 344072 | tf_op jit(solution)/shard_map/ppermute | solution.py:13
  409.6 8.8 %collective-permute-start = (bf16[1,16,3584]{2,1,0:T(8,128)(2,1)S(1)}, bf16[1,16,3584]{2,1,0:T(8,128)(2,1)S(1)}, u32[]{:S(2)}, u32[]{:S(2)}) collective-permute-start(bf16[1,16,3584]{2,1,0:T(8,128)(2,1)S(1)} %fusion.1), channel_id=1, source_target_pairs={{0,64},{64,128},{128,192},{192,256},{256,320},{320,384},{384,448},... | collective-permute-start | bytes 344072 | tf_op jit(solution)/shard_map/ppermute | solution.py:13
Sparse Core Ops, SparseCore 0:
  106.6 85.9 all-gather.2
  273.3 71.3 reduce-scatter.1

commit v2 on v1

--- a/solution.py
+++ b/solution.py
@@ -86,15 +86,18 @@
         "te,td->ed", weight_b, out_grad[0].astype(jnp.float32), precision=lax.Precision.HIGHEST
     )
     send_g = route_grad.astype(jnp.bfloat16)
-    payload = jnp.stack((send_f, send_x, send_g)).reshape(3, experts, capacity, width)
+    lanes = 128
+    payload = jnp.stack((send_f, send_x, send_g)).reshape(3, experts, -1, lanes)
     crossed = lax.all_to_all(payload, "eg", split_axis=1, concat_axis=1, tiled=True)
-    arrived = lax.all_gather(crossed, "ei", axis=1, tiled=False)
+    arrived = lax.all_gather(crossed, "p", axis=1, tiled=False)
+    arrived = lax.all_gather(arrived, "c", axis=2, tiled=False)
     rows = arrived.reshape(3, -1, width)
     out_f = expert_forward(rows[0], w_gate, w_up, w_down)
     out_b = expert_backward(rows[1], rows[2], w_gate, w_up, w_down)
-    parts = jnp.stack((out_f, out_b)).reshape((2,) + arrived.shape[1:])
-    summed = lax.psum_scatter(parts, "ei", scatter_dimension=1, tiled=True)
-    summed = summed.reshape(2, experts, capacity, width)
+    parts = jnp.stack((out_f, out_b)).reshape(2, arrived.shape[1], arrived.shape[2], experts, capacity, width)
+    summed = lax.psum_scatter(parts, "c", scatter_dimension=2, tiled=True)
+    summed = lax.psum_scatter(summed, "p", scatter_dimension=1, tiled=True)
+    summed = summed.reshape(2, experts, -1, lanes)
     home = lax.all_to_all(summed, "eg", split_axis=1, concat_axis=1, tiled=True)
     home = home.reshape(2, experts * capacity, width).astype(jnp.float32)
     layer_out = jnp.dot(weight_f, home[0], precision=lax.Precision.HIGHEST).astype(jnp.bfloat16)[
@@ -110,9 +113,10 @@
 
 def solution(mesh):
     pipe, expert = mesh.devices.shape
-    split = Mesh(mesh.devices.reshape(pipe, expert // GROUP, GROUP), ("pipe", "eg", "ei"))
-    rows = P("pipe", ("eg", "ei"), None)
-    cols = P("pipe", None, ("eg", "ei"))
+    shape = (pipe, expert // GROUP, GROUP // 2, 2)
+    split = Mesh(mesh.devices.reshape(shape), ("pipe", "eg", "p", "c"))
+    rows = P("pipe", ("eg", "p", "c"), None)
+    cols = P("pipe", None, ("eg", "p", "c"))
     placed = (rows, rows, rows, rows, rows, rows, rows, cols, cols, rows)
     return jax.shard_map(
         body,

time: 428 us -> 448 us (1.047)
  the two profiles are of different devices: /device:TPU:64 before, /device:TPU:96 now
where the time goes in v2:
time: 448 us; the launch traced here: 446 us
  waiting for transfers between devices  208 us (46%)
  blocking collectives  125 us (28%)
  local copies, waits for them, and re-layouts  50.8 us (11%)
  matrix products  30.7 us (7%)
  between operations  13.9 us (3%)
  other arithmetic  10.2 us (2%)
  starting transfers between devices  7.14 us (2%)
    all_gather x1, waiting for transfers between devices, body(): arrived = lax.all_gather(crossed, 'p', axis=1, tiled=False)  78.2 us
    all_to_all x1, blocking collectives, body(): lax.all_to_all(payload, 'eg', split_axis=1, concat_axis=1, tiled=True)  71.2 us
    reduce_scatter x1, waiting for transfers between devices, body(): summed = lax.psum_scatter(summed, 'p', scatter_dimension=1, tiled=True)  64.2 us
    all_to_all x1, blocking collectives, body(): home = lax.all_to_all(summed, 'eg', split_axis=1, concat_axis=1, tiled=True)  54 us
    all_gather x1, waiting for transfers between devices, body(): arrived = lax.all_gather(arrived, 'c', axis=2, tiled=False)  33.9 us
    reduce_scatter x1, waiting for transfers between devices, body(): summed = lax.psum_scatter(parts, 'c', scatter_dimension=2, tiled=True)  25.3 us
    another operation x3, local copies, waits for them, and re-layouts, body(): jnp.stack((out_f, out_b))  15.2 us
    squeeze x2, local copies, waits for them, and re-layouts, body(): out_b = expert_backward(rows[1], rows[2], w_gate, w_up, w_down)  12.4 us
  transfers between devices with their start and end apart: 6, of which 6 were waited for; matrix products, arithmetic and copies ran while one was open for 0% of the time, Pallas kernels for 0%

profile of v2, /device:TPU:96, one launch (start us, length us, event | category | flops | bytes accessed | tf_op | source)
XLA Modules:
  0.0 446.5 jit_solution(3369973888894020090)
XLA Ops:
  7.2 0.8 reduce_sum.78
  8.0 0.7 bitcast_divide_fusion.1
  8.7 0.7 reduce_sum.84
  9.4 0.7 bitcast_divide_fusion
  10.1 0.8 copy.58
  10.8 0.1 eq.56
  10.9 0.8 copy.60
  11.7 0.1 eq.63
  11.8 0.1 fusion.35
  11.8 0.1 reduce_window_sum.18
  11.9 0.2 select_reduce_fusion.1
  12.1 0.1 reduce_sum.82
  12.2 0.1 copy.61
  12.2 0.7 bitcast_add_fusion
  12.9 0.1 fusion.36
  13.0 0.1 reduce_window_sum.17
  13.1 0.2 select_reduce_fusion.3
  13.3 0.1 reduce_sum.77
  13.3 0.1 copy.59
  13.4 0.7 bitcast_add_fusion.1
  14.1 0.1 convert_reduce_fusion
  14.2 1.4 convolution_convert_fusion.1
  15.6 0.4 stack.23
  16.0 0.1 convert_reduce_fusion.1
  16.1 1.2 convolution_convert_fusion.3
  17.3 0.4 stack.21
  17.7 1.2 convolution_convert_fusion.2
  18.9 0.4 stack.22
  19.4 0.1 pad_maximum_fusion.1
  19.5 71.2 %all_to_all.10 = bf16[3,8,168,128]{3,2,0,1:T(8,128)(2,1)} all-to-all(bf16[3,8,168,128]{3,2,0,1:T(8,128)(2,1)S(1)} %pad_maximum_fusion.1), channel_id=1, replica_groups=mesh['pipe'=8,'eg'=8,'p'=4,'c'=2] {'eg'}, dimensions={1} | all-to-all | bytes 2064384 | tf_op jit(solution)/shard_map/all_to_all | solution.py:91
  90.7 78.2 %all-gather.5.cloned.1.call-done = bf16[3,32,168,128]{3,2,0,1:T(8,128)(2,1)} async-done(((bf16[3,8,168,128]{3,2,0,1:T(8,128)(2,1)}), bf16[3,32,168,128]{3,2,0,1:T(8,128)(2,1)}) %all-gather.5.cloned.1.call-update) | async-done | bytes 4128784 | tf_op jit(solution)/shard_map/all_gather | solution.py:92
  168.9 0.2 reduce-scatter.3.cloned.1.call-start
  169.1 33.9 %all-gather.7.cloned.1.call-done = bf16[3,4,16,168,128]{4,3,0,2,1:T(8,128)(2,1)} async-done(((bf16[3,4,8,168,128]{4,3,0,2,1:T(8,128)(2,1)}), bf16[3,4,16,168,128]{4,3,0,2,1:T(8,128)(2,1)}) %all-gather.7.cloned.1.call-update) | async-done | bytes 8257552 | tf_op jit(solution)/shard_map/all_gather | solution.py:93
  203.0 5.8 %fusion.42 = (bf16[1,4,16,168,128]{4,3,0,2,1:T(8,128)(2,1)}, bf16[1,4,16,168,128]{4,3,0,2,1:T(8,128)(2,1)}, bf16[1,4,16,168,128]{4,3,0,2,1:T(8,128)(2,1)}) fusion(bf16[3,4,16,168,128]{4,3,0,2,1:T(8,128)(2,1)} %all-gather.7.cloned.1.call-done), kind=kLoop, calls=%fused_computation.67 | loop fusion | bytes 16515072 | tf_op jit(solution)/shard_map/slice | solution.py:95
  208.8 6.2 %squeeze.44 = bf16[384,3584]{1,0:T(8,128)(2,1)} reshape(bf16[1,4,16,168,128]{4,3,0,2,1:T(8,128)(2,1)} %get-tuple-element.6) | data formatting | bytes 5505024 | tf_op jit(solution)/shard_map/squeeze | solution.py:95
  215.1 2.7 fusion.19
  217.8 6.4 %convolution_convert_fusion = bf16[384,3584]{1,0:T(8,128)(2,1)} fusion(bf16[384,3584]{1,0:T(8,128)(2,1)} %squeeze.44, bf16[1,128,3584]{2,1,0:T(8,128)(2,1)S(1)} %copy-done.3, bf16[1,3584,128]{2,1,0:T(8,128)(2,1)S(1)} %copy-done, f32[384,128]{1,0:T(8,128)S(1)} %fusion.19), kind=kOutput, calls=%fused_computation.3 | convolution fusion | flops 706314240 | bytes 7536640 | tf_op jit(solution)/shard_map/dot_general | solution.py:42
  224.2 5.4 %stack.25 = bf16[1,4,2,8,6,3584]{5,4,3,2,1,0:T(8,128)(2,1)} reshape(bf16[384,3584]{1,0:T(8,128)(2,1)} %convolution_convert_fusion) | data formatting | bytes 5505024 | tf_op jit(solution)/shard_map/stack | solution.py:97
  229.6 6.2 %squeeze.49 = bf16[384,3584]{1,0:T(8,128)(2,1)} reshape(bf16[1,4,16,168,128]{4,3,0,2,1:T(8,128)(2,1)} %get-tuple-element.8) | data formatting | bytes 5505024 | tf_op jit(solution)/shard_map/squeeze | solution.py:96
  235.8 2.6 fusion.17
  238.4 6.2 %squeeze.48 = bf16[384,3584]{1,0:T(8,128)(2,1)} reshape(bf16[1,4,16,168,128]{4,3,0,2,1:T(8,128)(2,1)} %get-tuple-element.7) | data formatting | bytes 5505024 | tf_op jit(solution)/shard_map/squeeze | solution.py:96
  244.6 2.6 fusion.8
  247.2 7.2 %fusion.7 = f32[384,3584]{1,0:T(8,128)} fusion(f32[384,128]{1,0:T(8,128)S(1)} %fusion.8, bf16[384,3584]{1,0:T(8,128)(2,1)} %squeeze.49, bf16[1,3584,128]{2,1,0:T(8,128)(2,1)S(1)} %copy-done, bf16[1,3584,128]{2,1,0:T(8,128)(2,1)S(1)} %copy-done.2, f32[384,128]{1,0:T(8,128)S(1)} %fusion.17), kind=kOutput, calls=%fused_computation.17 | convolution fusion | flops 705134592 | bytes 10485760 | tf_op jit(solution)/shard_map/dot_general | solution.py:54
  254.4 5.0 %fusion = bf16[384,3584]{1,0:T(8,128)(2,1)} fusion(f32[384,3584]{1,0:T(8,128)} %fusion.7, bf16[1,3584,128]{2,1,0:T(8,128)(2,1)S(1)} %copy-done, f32[384,128]{1,0:T(8,128)S(1)} %fusion.8, f32[384,128]{1,0:T(8,128)S(1)} %fusion.17), kind=kOutput, calls=%fused_computation.2 | convolution fusion | flops 355368960 | bytes 9568256 | tf_op jit(solution)/shard_map/dot_general | solution.py:57
  259.4 5.4 %stack.26 = bf16[1,4,2,8,6,3584]{5,4,3,2,1,0:T(8,128)(2,1)} reshape(bf16[384,3584]{1,0:T(8,128)(2,1)} %fusion) | data formatting | bytes 5505024 | tf_op jit(solution)/shard_map/stack | solution.py:97
  264.8 5.1 %pad_maximum_fusion = bf16[2,4,2,8,6,3584]{5,4,3,2,1,0:T(8,128)(2,1)S(1)} fusion(bf16[1,4,2,8,6,3584]{5,4,3,2,1,0:T(8,128)(2,1)} %stack.26, bf16[1,4,2,8,6,3584]{5,4,3,2,1,0:T(8,128)(2,1)} %stack.25), kind=kLoop, calls=%fused_computation | loop fusion | flops 2752512 | bytes 11010048 | tf_op jit(solution)/shard_map/stack | solution.py:97
  269.9 4.4 copy.65
  274.3 0.0 reduce-scatter.5.cloned.1.call-start
  274.3 25.3 %reduce-scatter.3.cloned.1.call-done = bf16[2,4,1,8,6,3584]{5,3,4,1,0,2:T(8,128)(2,1)} async-done(((bf16[2,4,2,8,6,3584]{5,3,4,1,0,2:T(8,128)(2,1)}), bf16[2,4,1,8,6,3584]{5,3,4,1,0,2:T(8,128)(2,1)}) %reduce-scatter.3.cloned.1.call-update) | async-done | bytes 2752528 | tf_op jit(solution)/shard_map/reduce_scatter | solution.py:98
  299.7 3.5 copy.66
  303.2 64.2 %reduce-scatter.5.cloned.1.call-done = bf16[2,1,1,8,6,3584]{5,3,4,2,0,1:T(8,128)(2,1)} async-done(((bf16[2,4,1,8,6,3584]{5,3,4,2,0,1:T(8,128)(2,1)}), bf16[2,1,1,8,6,3584]{5,3,4,2,0,1:T(8,128)(2,1)}) %reduce-scatter.5.cloned.1.call-update) | async-done | bytes 688144 | tf_op jit(solution)/shard_map/reduce_scatter | solution.py:99
  367.4 1.3 copy.69
  368.7 0.8 reshape.106
  369.6 54.0 %all_to_all.11 = bf16[2,8,168,128]{3,2,0,1:T(8,128)(2,1)S(1)} all-to-all(bf16[2,8,168,128]{3,2,0,1:T(8,128)(2,1)S(1)} %reshape.106), channel_id=1, replica_groups=mesh['pipe'=8,'eg'=8,'p'=4,'c'=2] {'eg'}, dimensions={1} | all-to-all | bytes 1376256 | tf_op jit(solution)/shard_map/all_to_all | solution.py:101
  423.6 0.4 squeeze.51
  424.0 0.3 fusion.2
  424.3 4.9 %collective-permute-start.1 = (bf16[1,16,3584]{2,1,0:T(8,128)(2,1)S(1)}, bf16[1,16,3584]{2,1,0:T(8,128)(2,1)S(1)}, u32[]{:S(2)}, u32[]{:S(2)}) collective-permute-start(bf16[1,16,3584]{2,1,0:T(8,128)(2,1)S(1)} %fusion.2), channel_id=1, source_target_pairs={{0,448},{64,0},{128,64},{192,128},{256,192},{320,256},{384,320},{4... | collective-permute-start | bytes 344072 | tf_op jit(solution)/shard_map/ppermute | solution.py:13
  429.2 0.4 squeeze.50
  429.6 0.3 fusion.1
  429.8 1.9 collective-permute-start
  431.8 0.2 collective-permute-done.1
  432.0 6.6 %collective-permute-done = bf16[1,16,3584]{2,1,0:T(8,128)(2,1)S(1)} collective-permute-done((bf16[1,16,3584]{2,1,0:T(8,128)(2,1)S(1)}, bf16[1,16,3584]{2,1,0:T(8,128)(2,1)S(1)}, u32[]{:S(2)}, u32[]{:S(2)}) %collective-permute-start) | collective-permute-done | bytes 114720 | tf_op jit(solution)/shard_map/ppermute | solution.py:13
  438.6 0.6 copy.73
  439.3 0.6 copy.74
  (15 shorter events, 0.2 us)
Async XLA Ops:
  7.2 210.6 %copy-start = (bf16[1,3584,128]{2,1,0:T(8,128)(2,1)S(1)}, bf16[1,3584,128]{2,1,0:T(8,128)(2,1)}, u32[]{:S(2)}) copy-start(bf16[1,3584,128]{2,1,0:T(8,128)(2,1)} %param.18) | copy-start | bytes 2752516
  7.2 161.7 %all-gather.5.cloned.1.call-start = ((), (), s32[]{:S(2)}) async-start(), calls=%async_computation.6 | async-start | bytes 5160960 | tf_op jit(solution)/shard_map/all_gather | solution.py:92
  90.7 112.3 %all-gather.7.cloned.1.call-start = ((), (), s32[]{:S(2)}) async-start(), calls=%async_computation.7 | async-start | bytes 12386304 | tf_op jit(solution)/shard_map/all_gather | solution.py:93
  168.9 130.8 %reduce-scatter.3.cloned.1.call-start = ((), (), s32[]{:S(2)}) async-start(), calls=%async_computation.4 | async-start | bytes 8257536 | tf_op jit(solution)/shard_map/reduce_scatter | solution.py:98
  208.8 6.3 %copy-start.2 = (bf16[1,3584,128]{2,1,0:T(8,128)(2,1)S(1)}, bf16[1,3584,128]{2,1,0:T(8,128)(2,1)}, u32[]{:S(2)}) copy-start(bf16[1,3584,128]{2,1,0:T(8,128)(2,1)} %param.17) | copy-start | bytes 2752516
  215.1 2.7 copy-start.3
  274.3 93.1 %reduce-scatter.5.cloned.1.call-start = ((), (), s32[]{:S(2)}) async-start(), calls=%async_computation.5 | async-start | bytes 3440640 | tf_op jit(solution)/shard_map/reduce_scatter | solution.py:99
  368.7 71.2 %copy-start.1 = (bf16[1,3584,128]{2,1,0:T(8,128)(2,1)S(1)}, bf16[1,3584,128]{2,1,0:T(8,128)(2,1)}, u32[]{:S(2)}) copy-start(bf16[1,3584,128]{2,1,0:T(8,128)(2,1)} %param.18) | copy-start | bytes 2752516
  424.3 7.7 %collective-permute-start.1 = (bf16[1,16,3584]{2,1,0:T(8,128)(2,1)S(1)}, bf16[1,16,3584]{2,1,0:T(8,128)(2,1)S(1)}, u32[]{:S(2)}, u32[]{:S(2)}) collective-permute-start(bf16[1,16,3584]{2,1,0:T(8,128)(2,1)S(1)} %fusion.2), channel_id=1, source_target_pairs={{0,448},{64,0},{128,64},{192,128},{256,192},{320,256},{384,320},{4... | collective-permute-start | bytes 344072 | tf_op jit(solution)/shard_map/ppermute | solution.py:13
  429.8 8.8 %collective-permute-start = (bf16[1,16,3584]{2,1,0:T(8,128)(2,1)S(1)}, bf16[1,16,3584]{2,1,0:T(8,128)(2,1)S(1)}, u32[]{:S(2)}, u32[]{:S(2)}) collective-permute-start(bf16[1,16,3584]{2,1,0:T(8,128)(2,1)S(1)} %fusion.1), channel_id=1, source_target_pairs={{0,64},{64,128},{128,192},{192,256},{256,320},{320,384},{384,448},... | collective-permute-start | bytes 344072 | tf_op jit(solution)/shard_map/ppermute | solution.py:13
Sparse Core Ops, SparseCore 0:
  90.8 78.0 all-gather.4
  170.9 32.0 all-gather.6
  274.4 25.2 reduce-scatter.2
  303.4 63.9 reduce-scatter.4

commit v3 on v1

--- a/solution.py
+++ b/solution.py
@@ -35,29 +35,29 @@
     return slots.astype(jnp.bfloat16)
 
 
-def expert_forward(flat, w_gate, w_up, w_down):
-    first = jnp.dot(flat, w_gate, preferred_element_type=jnp.float32)
-    second = jnp.dot(flat, w_up, preferred_element_type=jnp.float32)
-    hidden = (jax.nn.silu(first) * second).astype(jnp.bfloat16)
-    return jnp.dot(hidden, w_down, preferred_element_type=jnp.float32).astype(jnp.bfloat16)
-
-
-def expert_backward(flat, grads, w_gate, w_up, w_down):
-    first = jnp.dot(flat, w_gate, preferred_element_type=jnp.float32)
-    second = jnp.dot(flat, w_up, preferred_element_type=jnp.float32)
+def expert_pair(rows, grads, w_gate, w_up, w_down):
+    count = grads.shape[0]
+    hid = w_gate.shape[1]
+    both = jnp.dot(rows, jnp.concatenate((w_gate, w_up), axis=1), preferred_element_type=jnp.float32)
+    first, second = both[:, :hid], both[:, hid:]
+    hidden = (jax.nn.silu(first[:count]) * second[:count]).astype(jnp.bfloat16)
     d_hidden = lax.dot_general(
         grads, w_down, (((1,), (1,)), ((), ())), preferred_element_type=jnp.float32
     )
-    sigm = 1.0 / (1.0 + jnp.exp(-first))
-    d_first = (d_hidden * second * sigm * (1.0 + first * (1.0 - sigm))).astype(jnp.bfloat16)
-    d_second = (d_hidden * first * sigm).astype(jnp.bfloat16)
-    back = lax.dot_general(
-        d_first, w_gate, (((1,), (1,)), ((), ())), preferred_element_type=jnp.float32
+    a, b = first[count:], second[count:]
+    sigm = 1.0 / (1.0 + jnp.exp(-a))
+    d_first = (d_hidden * b * sigm * (1.0 + a * (1.0 - sigm))).astype(jnp.bfloat16)
+    d_second = (d_hidden * a * sigm).astype(jnp.bfloat16)
+    zero = jnp.zeros_like(hidden)
+    left = jnp.concatenate(
+        (
+            jnp.concatenate((hidden, zero, zero), axis=1),
+            jnp.concatenate((zero, d_first, d_second), axis=1),
+        ),
+        axis=0,
     )
-    back = back + lax.dot_general(
-        d_second, w_up, (((1,), (1,)), ((), ())), preferred_element_type=jnp.float32
-    )
-    return back.astype(jnp.bfloat16)
+    right = jnp.concatenate((w_down, w_gate.T, w_up.T), axis=0)
+    return jnp.dot(left, right, preferred_element_type=jnp.float32).astype(jnp.bfloat16)
 
 
 def body(
@@ -86,15 +86,17 @@
         "te,td->ed", weight_b, out_grad[0].astype(jnp.float32), precision=lax.Precision.HIGHEST
     )
     send_g = route_grad.astype(jnp.bfloat16)
-    payload = jnp.stack((send_f, send_x, send_g)).reshape(3, experts, capacity, width)
+    lanes = 128
+    payload = jnp.stack((send_f, send_x, send_g)).reshape(3, experts, -1, lanes)
     crossed = lax.all_to_all(payload, "eg", split_axis=1, concat_axis=1, tiled=True)
+    crossed = crossed.reshape(3, experts, capacity, width).transpose(0, 2, 1, 3)
     arrived = lax.all_gather(crossed, "ei", axis=1, tiled=False)
     rows = arrived.reshape(3, -1, width)
-    out_f = expert_forward(rows[0], w_gate, w_up, w_down)
-    out_b = expert_backward(rows[1], rows[2], w_gate, w_up, w_down)
-    parts = jnp.stack((out_f, out_b)).reshape((2,) + arrived.shape[1:])
+    parts = expert_pair(rows[:2].reshape(-1, width), rows[2], w_gate, w_up, w_down)
+    parts = parts.reshape((2,) + arrived.shape[1:])
     summed = lax.psum_scatter(parts, "ei", scatter_dimension=1, tiled=True)
-    summed = summed.reshape(2, experts, capacity, width)
+    summed = summed.reshape(2, capacity, experts, width).transpose(0, 2, 1, 3)
+    summed = summed.reshape(2, experts, -1, lanes)
     home = lax.all_to_all(summed, "eg", split_axis=1, concat_axis=1, tiled=True)
     home = home.reshape(2, experts * capacity, width).astype(jnp.float32)
     layer_out = jnp.dot(weight_f, home[0], precision=lax.Precision.HIGHEST).astype(jnp.bfloat16)[

time: 428 us -> 364 us (0.85)
  local copies, waits for them, and re-layouts: 58.9 us -> 20.9 us
  matrix products: 30 us -> 9.02 us
  waiting for transfers between devices: 164 us -> 182 us
  blocking collectives: 142 us -> 126 us
  other arithmetic: 10.4 us -> 5.04 us
    dot_general x6 -> x3, matrix products: 26.7 us -> 5.7 us  [the longest x1 3.23 us: expert_pair(): jnp.dot(left, right, preferred_element_type=jnp.float32)]
    reduce_scatter x1, waiting for transfers between devices: 71.5 us -> 88.8 us  [body(): summed = lax.psum_scatter(parts, 'ei', scatter_dimension=1, tiled=True)]
    squeeze x3 -> x0, local copies, waits for them, and re-layouts: 16.5 us -> none  [the longest x2 11 us: body(): out_b = expert_backward(rows[1], rows[2], w_gate, w_up, w_down)]
    all_to_all x1, blocking collectives: 87.1 us -> 70.8 us  [body(): lax.all_to_all(payload, 'eg', split_axis=1, concat_axis=1, tiled=True)]
    slice x4 -> x2, local copies, waits for them, and re-layouts: 17 us -> 2.56 us  [body(): rows[:2].reshape(-1, width)]
    another operation x7 -> x3, local copies, waits for them, and re-layouts: 15.6 us -> 1.34 us  [body(): payload = jnp.stack((send_f, send_x, send_g)).reshape(3, experts, -1, lanes)]
    reshape x1 -> x4, local copies, waits for them, and re-layouts: 1.81 us -> 8.31 us  [the longest x1 5.11 us: body(): parts = parts.reshape((2,) + arrived.shape[1:])]
    another operation x2 -> x1, other arithmetic: 5.44 us -> 0.11 us  [body(): payload = jnp.stack((send_f, send_x, send_g)).reshape(3, experts, -1, lanes)]
where the time goes in v3:
time: 364 us
  waiting for transfers between devices  182 us (50%)
  blocking collectives  126 us (35%)
  local copies, waits for them, and re-layouts  20.9 us (6%)
  between operations  14.3 us (4%)
  matrix products  9.02 us (2%)
  starting transfers between devices  6.65 us (2%)
  other arithmetic  5.04 us (1%)
    reduce_scatter x1, waiting for transfers between devices, body(): summed = lax.psum_scatter(parts, 'ei', scatter_dimension=1, tiled=True)  88.8 us
    all_gather x1, waiting for transfers between devices, body(): arrived = lax.all_gather(crossed, 'ei', axis=1, tiled=False)  86.4 us
    all_to_all x1, blocking collectives, body(): lax.all_to_all(payload, 'eg', split_axis=1, concat_axis=1, tiled=True)  70.8 us
    all_to_all x1, blocking collectives, body(): home = lax.all_to_all(summed, 'eg', split_axis=1, concat_axis=1, tiled=True)  54.7 us
  transfers between devices with their start and end apart: 4, of which 4 were waited for; matrix products, arithmetic and copies ran while one was open for 0% of the time, Pallas kernels for 0%

profile of v3, /device:TPU:64, one launch (start us, length us, event | category | flops | bytes accessed | tf_op | source)
XLA Modules:
  0.0 363.7 jit_solution(17045322509368653463)
XLA Ops:
  7.2 0.0 copy-start
  7.2 0.0 all-gather.3.cloned.1.call-start
  7.2 0.8 copy.62
  8.0 0.1 eq.63
  8.1 0.1 fusion.30
  8.1 0.1 reduce_window_sum.18
  8.2 0.2 select_reduce_fusion.1
  8.4 0.1 reduce_sum.82
  8.5 0.1 copy.63
  8.6 0.7 bitcast_add_fusion
  9.3 0.7 reduce_sum.84
  10.0 0.7 bitcast_divide_fusion
  10.6 0.1 convert_reduce_fusion
  10.7 0.0 copy-done
  10.7 0.3 convolution_convert_fusion.2
  11.0 0.4 stack.13
  11.4 1.4 convolution_convert_fusion.1
  12.8 0.4 stack.14
  13.3 0.8 copy.60
  14.0 0.1 eq.56
  14.1 0.1 fusion.31
  14.2 0.1 reduce_window_sum.17
  14.3 0.2 select_reduce_fusion.3
  14.4 0.1 reduce_sum.77
  14.5 0.1 copy.61
  14.6 0.7 bitcast_add_fusion.1
  15.3 0.7 reduce_sum.78
  16.0 0.7 bitcast_divide_fusion.1
  16.7 0.1 convert_reduce_fusion.1
  16.8 1.2 convolution_convert_fusion.3
  17.9 0.4 stack.12
  18.4 0.1 pad_maximum_fusion
  18.5 70.8 %all_to_all.10 = bf16[3,8,168,128]{3,2,0,1:T(8,128)(2,1)S(1)} all-to-all(bf16[3,8,168,128]{3,2,0,1:T(8,128)(2,1)S(1)} %pad_maximum_fusion), channel_id=1, replica_groups=mesh['pipe'=8,'eg'=8,'ei'=8] {'eg'}, dimensions={1} | all-to-all | bytes 2064384 | tf_op jit(solution)/shard_map/all_to_all | solution.py:91
  89.4 0.1 copy.67
  89.5 1.2 reshape.102
  90.6 1.3 copy.68
  92.0 0.0 all-gather.3.cloned.1.call-update
  92.0 0.0 reduce-scatter.2.cloned.1.call-start
  92.1 0.5 copy.70
  92.6 0.5 copy.71
  93.1 86.4 %all-gather.3.cloned.1.call-done = bf16[3,48,8,3584]{3,2,0,1:T(8,128)(2,1)} async-done(((bf16[3,6,8,3584]{3,2,0,1:T(8,128)(2,1)}), bf16[3,48,8,3584]{3,2,0,1:T(8,128)(2,1)}) %all-gather.3.cloned.1.call-update) | async-done | bytes 8257552 | tf_op jit(solution)/shard_map/all_gather | solution.py:93
  179.5 2.6 slice-done.2
  182.1 0.4 copy.78
  182.5 1.6 fusion.8
  184.1 0.1 slice-done
  184.2 1.4 slice-done.1
  185.6 0.2 copy-done.3
  185.8 0.9 fusion.25
  186.7 3.2 convolution_convert_fusion
  189.9 5.1 %copy.75 = bf16[2,8,6,8,3584]{4,2,3,0,1:T(8,128)(2,1)} copy(bf16[2,8,6,8,3584]{4,3,2,1,0:T(8,128)(2,1)S(1)} %bitcast.67) | data formatting | bytes 11010048 | tf_op jit(solution)/shard_map/reshape | solution.py:96
  195.0 0.0 reduce-scatter.2.cloned.1.call-update
  195.0 88.8 %reduce-scatter.2.cloned.1.call-done = bf16[2,1,6,8,3584]{4,2,3,0,1:T(8,128)(2,1)} async-done(((bf16[2,8,6,8,3584]{4,2,3,0,1:T(8,128)(2,1)}), bf16[2,1,6,8,3584]{4,2,3,0,1:T(8,128)(2,1)}) %reduce-scatter.2.cloned.1.call-update) | async-done | bytes 688144 | tf_op jit(solution)/shard_map/reduce_scatter | solution.py:97
  283.9 2.0 reshape.106
  285.9 54.7 %all_to_all.11 = bf16[2,8,168,128]{3,2,0,1:T(8,128)(2,1)S(1)} all-to-all(bf16[2,8,168,128]{3,2,0,1:T(8,128)(2,1)S(1)} %copy.76), channel_id=1, replica_groups=mesh['pipe'=8,'eg'=8,'ei'=8] {'eg'}, dimensions={1} | all-to-all | bytes 1376256 | tf_op jit(solution)/shard_map/all_to_all | solution.py:100
  340.7 0.4 squeeze.43
  341.1 0.3 fusion.1
  341.4 4.7 %collective-permute-start.1 = (bf16[1,16,3584]{2,1,0:T(8,128)(2,1)S(1)}, bf16[1,16,3584]{2,1,0:T(8,128)(2,1)S(1)}, u32[]{:S(2)}, u32[]{:S(2)}) collective-permute-start(bf16[1,16,3584]{2,1,0:T(8,128)(2,1)S(1)} %fusion.1), channel_id=1, source_target_pairs={{0,448},{64,0},{128,64},{192,128},{256,192},{320,256},{384,320},{4... | collective-permute-start | bytes 344072 | tf_op jit(solution)/shard_map/ppermute | solution.py:13
  346.1 0.4 squeeze.42
  346.5 0.3 fusion
  346.7 1.9 collective-permute-start
  348.7 0.5 collective-permute-done.1
  349.1 6.4 %collective-permute-done = bf16[1,16,3584]{2,1,0:T(8,128)(2,1)S(1)} collective-permute-done((bf16[1,16,3584]{2,1,0:T(8,128)(2,1)S(1)}, bf16[1,16,3584]{2,1,0:T(8,128)(2,1)S(1)}, u32[]{:S(2)}, u32[]{:S(2)}) %collective-permute-start) | collective-permute-done | bytes 114720 | tf_op jit(solution)/shard_map/ppermute | solution.py:13
  355.5 0.6 copy.82
  356.2 0.6 copy.83
  (12 shorter events, 0.1 us)
Async XLA Ops:
  7.2 3.6 copy-start
  7.2 172.3 %all-gather.3.cloned.1.call-start = ((), (), s32[]{:S(2)}) async-start(), calls=%async_computation.4 | async-start | bytes 9289728 | tf_op jit(solution)/shard_map/all_gather | solution.py:93
  89.4 2.6 copy-start.1
  90.6 2.0 copy-start.2
  92.0 191.9 %reduce-scatter.2.cloned.1.call-start = ((), (), s32[]{:S(2)}) async-start(), calls=%async_computation.3 | async-start | bytes 8257536 | tf_op jit(solution)/shard_map/reduce_scatter | solution.py:97
  179.5 2.6 slice-start.2
  182.1 2.2 slice-start
  182.5 3.1 slice-start.1
  182.5 3.3 copy-start.3
  341.4 7.7 %collective-permute-start.1 = (bf16[1,16,3584]{2,1,0:T(8,128)(2,1)S(1)}, bf16[1,16,3584]{2,1,0:T(8,128)(2,1)S(1)}, u32[]{:S(2)}, u32[]{:S(2)}) collective-permute-start(bf16[1,16,3584]{2,1,0:T(8,128)(2,1)S(1)} %fusion.1), channel_id=1, source_target_pairs={{0,448},{64,0},{128,64},{192,128},{256,192},{320,256},{384,320},{4... | collective-permute-start | bytes 344072 | tf_op jit(solution)/shard_map/ppermute | solution.py:13
  346.7 8.8 %collective-permute-start = (bf16[1,16,3584]{2,1,0:T(8,128)(2,1)S(1)}, bf16[1,16,3584]{2,1,0:T(8,128)(2,1)S(1)}, u32[]{:S(2)}, u32[]{:S(2)}) collective-permute-start(bf16[1,16,3584]{2,1,0:T(8,128)(2,1)S(1)} %fusion), channel_id=1, source_target_pairs={{0,64},{64,128},{128,192},{192,256},{256,320},{320,384},{384,448},... | collective-permute-start | bytes 344072 | tf_op jit(solution)/shard_map/ppermute | solution.py:13
Sparse Core Ops, SparseCore 0:
  92.1 87.3 all-gather.2
  195.2 88.6 reduce-scatter.1

commit v4 on v3

--- a/solution.py
+++ b/solution.py
@@ -35,29 +35,42 @@
     return slots.astype(jnp.bfloat16)
 
 
-def expert_pair(rows, grads, w_gate, w_up, w_down):
-    count = grads.shape[0]
+def expert_forward(rows, w_gate, w_up, w_down):
+    first = jnp.dot(rows, w_gate, preferred_element_type=jnp.float32)
+    second = jnp.dot(rows, w_up, preferred_element_type=jnp.float32)
+    hidden = (jax.nn.silu(first) * second).astype(jnp.bfloat16)
+    return jnp.dot(hidden, w_down, preferred_element_type=jnp.float32).astype(jnp.bfloat16)
+
+
+def expert_backward(rows, grads, w_gate, w_up, w_down):
     hid = w_gate.shape[1]
     both = jnp.dot(rows, jnp.concatenate((w_gate, w_up), axis=1), preferred_element_type=jnp.float32)
-    first, second = both[:, :hid], both[:, hid:]
-    hidden = (jax.nn.silu(first[:count]) * second[:count]).astype(jnp.bfloat16)
+    a, b = both[:, :hid], both[:, hid:]
     d_hidden = lax.dot_general(
         grads, w_down, (((1,), (1,)), ((), ())), preferred_element_type=jnp.float32
     )
-    a, b = first[count:], second[count:]
     sigm = 1.0 / (1.0 + jnp.exp(-a))
     d_first = (d_hidden * b * sigm * (1.0 + a * (1.0 - sigm))).astype(jnp.bfloat16)
     d_second = (d_hidden * a * sigm).astype(jnp.bfloat16)
-    zero = jnp.zeros_like(hidden)
-    left = jnp.concatenate(
-        (
-            jnp.concatenate((hidden, zero, zero), axis=1),
-            jnp.concatenate((zero, d_first, d_second), axis=1),
-        ),
-        axis=0,
-    )
-    right = jnp.concatenate((w_down, w_gate.T, w_up.T), axis=0)
+    left = jnp.concatenate((d_first, d_second), axis=1)
+    right = jnp.concatenate((w_gate.T, w_up.T), axis=0)
     return jnp.dot(left, right, preferred_element_type=jnp.float32).astype(jnp.bfloat16)
+
+
+def dispatch(payload, capacity, width):
+    kinds, experts = payload.shape[:2]
+    crossed = lax.all_to_all(payload, "eg", split_axis=1, concat_axis=1, tiled=True)
+    crossed = crossed.reshape(kinds, experts, capacity, width).transpose(0, 2, 1, 3)
+    return lax.all_gather(crossed, "ei", axis=1, tiled=False)
+
+
+def collect(parts, lanes):
+    kinds, _, capacity, experts, width = parts.shape
+    summed = lax.psum_scatter(parts, "ei", scatter_dimension=1, tiled=True)
+    summed = summed.reshape(kinds, capacity, experts, width).transpose(0, 2, 1, 3)
+    summed = summed.reshape(kinds, experts, -1, lanes)
+    home = lax.all_to_all(summed, "eg", split_axis=1, concat_axis=1, tiled=True)
+    return home.reshape(kinds, experts * capacity, width).astype(jnp.float32)
 
 
 def body(
@@ -87,18 +100,15 @@
     )
     send_g = route_grad.astype(jnp.bfloat16)
     lanes = 128
-    payload = jnp.stack((send_f, send_x, send_g)).reshape(3, experts, -1, lanes)
-    crossed = lax.all_to_all(payload, "eg", split_axis=1, concat_axis=1, tiled=True)
-    crossed = crossed.reshape(3, experts, capacity, width).transpose(0, 2, 1, 3)
-    arrived = lax.all_gather(crossed, "ei", axis=1, tiled=False)
-    rows = arrived.reshape(3, -1, width)
-    parts = expert_pair(rows[:2].reshape(-1, width), rows[2], w_gate, w_up, w_down)
-    parts = parts.reshape((2,) + arrived.shape[1:])
-    summed = lax.psum_scatter(parts, "ei", scatter_dimension=1, tiled=True)
-    summed = summed.reshape(2, capacity, experts, width).transpose(0, 2, 1, 3)
-    summed = summed.reshape(2, experts, -1, lanes)
-    home = lax.all_to_all(summed, "eg", split_axis=1, concat_axis=1, tiled=True)
-    home = home.reshape(2, experts * capacity, width).astype(jnp.float32)
+    arrived_b = dispatch(jnp.stack((send_x, send_g)).reshape(2, experts, -1, lanes), capacity, width)
+    arrived_f = dispatch(send_f.reshape(1, experts, -1, lanes), capacity, width)
+    grid = arrived_f.shape
+    rows_b = arrived_b.reshape(2, -1, width)
+    out_b = expert_backward(rows_b[0], rows_b[1], w_gate, w_up, w_down)
+    out_f = expert_forward(arrived_f.reshape(-1, width), w_gate, w_up, w_down)
+    home_b = collect(out_b.reshape(grid), lanes)
+    home_f = collect(out_f.reshape(grid), lanes)
+    home = (home_f[0], home_b[0])
     layer_out = jnp.dot(weight_f, home[0], precision=lax.Precision.HIGHEST).astype(jnp.bfloat16)[
         None
     ]

time: 364 us -> 372 us (1.022)
  the two profiles are of different devices: /device:TPU:64 before, /device:TPU:58 now
where the time goes in v4:
time: 372 us; the launch traced here: 371 us
  waiting for transfers between devices  190 us (51%)
  blocking collectives  93.5 us (25%)
  starting transfers between devices  34.8 us (9%)
  local copies, waits for them, and re-layouts  20.2 us (5%)
  matrix products  16 us (4%)
  between operations  14 us (4%)
    reduce_scatter x2, waiting for transfers between devices, collect(): summed = lax.psum_scatter(parts, 'ei', scatter_dimension=1, tiled=True)  98.6 us
    all_to_all x2, blocking collectives, dispatch(): lax.all_to_all(payload, 'eg', split_axis=1, concat_axis=1, tiled=True)  93.5 us
    all_gather x2, waiting for transfers between devices, dispatch(): return lax.all_gather(crossed, 'ei', axis=1, tiled=False)  63.9 us
    all_to_all x2, starting transfers between devices, collect(): home = lax.all_to_all(summed, 'eg', split_axis=1, concat_axis=1, tiled=True)  28 us
    all_to_all x2, waiting for transfers between devices, collect(): home = lax.all_to_all(summed, 'eg', split_axis=1, concat_axis=1, tiled=True)  21.7 us
  transfers between devices with their start and end apart: 8, of which 6 were waited for; matrix products, arithmetic and copies ran while one was open for 8% of the time, Pallas kernels for 0%

profile of v4, /device:TPU:58, one launch (start us, length us, event | category | flops | bytes accessed | tf_op | source)
XLA Modules:
  0.0 371.4 jit_solution(8991811843493066361)
XLA Ops:
  7.2 0.0 all-gather.5.cloned.1.call-start
  7.3 0.9 copy.65
  8.1 0.1 eq.56
  8.2 0.1 fusion.29
  8.3 0.1 reduce_window_sum.17
  8.4 0.2 select_reduce_fusion.3
  8.5 0.1 reduce_sum.77
  8.6 0.1 copy.66
  8.7 0.7 bitcast_add_fusion.1
  9.4 0.7 reduce_sum.78
  10.1 0.7 bitcast_divide_fusion.1
  10.8 0.1 convert_reduce_fusion.1
  10.9 1.2 convolution_convert_fusion.4
  12.0 0.4 reshape.114
  12.5 43.1 %all_to_all.20 = bf16[1,8,168,128]{3,2,0,1:T(8,128)(2,1)S(1)} all-to-all(bf16[1,8,168,128]{3,2,0,1:T(8,128)(2,1)S(1)} %bitcast.97), channel_id=1, replica_groups=mesh['pipe'=8,'eg'=8,'ei'=8] {'eg'}, dimensions={1} | all-to-all | bytes 688128 | tf_op jit(solution)/shard_map/all_to_all | solution.py:62
  55.6 0.4 reshape.115
  56.0 0.9 copy.68
  56.9 0.0 all-gather.5.cloned.1.call-update
  56.9 0.0 all-gather.7.cloned.1.call-start
  57.0 0.1 copy.71
  57.1 0.1 eq.63
  57.2 0.1 fusion.28
  57.2 0.1 reduce_window_sum.18
  57.3 0.2 select_reduce_fusion.1
  57.5 0.1 reduce_sum.82
  57.5 0.1 copy.72
  57.7 0.1 select_reduce_fusion
  57.8 0.5 convolution_convert_fusion.2
  58.2 0.4 stack.10
  58.7 0.3 convolution_convert_fusion.3
  59.0 0.4 stack.9
  59.4 0.1 pad_maximum_fusion
  59.5 50.4 %all_to_all.21 = bf16[2,8,168,128]{3,2,0,1:T(8,128)(2,1)S(1)} all-to-all(bf16[2,8,168,128]{3,2,0,1:T(8,128)(2,1)S(1)} %pad_maximum_fusion), channel_id=1, replica_groups=mesh['pipe'=8,'eg'=8,'ei'=8] {'eg'}, dimensions={1} | all-to-all | bytes 1376256 | tf_op jit(solution)/shard_map/all_to_all | solution.py:62
  110.0 0.7 reshape.120
  110.7 1.1 copy.76
  111.8 0.0 all-gather.7.cloned.1.call-update
  111.8 0.0 reduce-scatter.3.cloned.1.call-start
  111.9 6.7 %all-gather.5.cloned.1.call-done = bf16[8,6,8,3584]{3,2,1,0:T(8,128)(2,1)} async-done(((bf16[1,6,8,3584]{3,2,1,0:T(8,128)(2,1)}), bf16[8,6,8,3584]{3,2,1,0:T(8,128)(2,1)}) %all-gather.5.cloned.1.call-update) | async-done | bytes 2752528 | tf_op jit(solution)/shard_map/all_gather | solution.py:64
  118.6 2.6 fusion.36
  121.3 6.3 %convolution_convert_fusion.1 = bf16[384,3584]{1,0:T(8,128)(2,1)} fusion(bf16[384,3584]{1,0:T(8,128)(2,1)} %bitcast.90, bf16[1,128,3584]{2,1,0:T(8,128)(2,1)S(1)} %copy-done, f32[384,128]{1,0:T(8,128)S(1)} %fusion.36, bf16[1,3584,128]{2,1,0:T(8,128)(2,1)S(1)} %copy-done.2), kind=kOutput, calls=%fused_computation.1 | convolution fusion | flops 706314240 | bytes 7536640 | tf_op jit(solution)/shard_map/dot_general | solution.py:42
  127.6 4.5 %copy.69 = bf16[1,8,6,8,3584]{4,2,3,1,0:T(8,128)(2,1)} copy(bf16[1,8,6,8,3584]{4,3,2,1,0:T(8,128)(2,1)} %bitcast.91) | data formatting | bytes 5505024 | tf_op jit(solution)/shard_map/reshape | solution.py:110
  132.2 0.0 reduce-scatter.5.cloned.1.call-start
  132.2 57.2 %all-gather.7.cloned.1.call-done = bf16[2,48,8,3584]{3,2,0,1:T(8,128)(2,1)} async-done(((bf16[2,6,8,3584]{3,2,0,1:T(8,128)(2,1)}), bf16[2,48,8,3584]{3,2,0,1:T(8,128)(2,1)}) %all-gather.7.cloned.1.call-update) | async-done | bytes 5505040 | tf_op jit(solution)/shard_map/all_gather | solution.py:64
  189.4 2.8 fusion.2
  192.2 0.6 copy-done.7
  192.8 0.9 fusion.15
  193.6 0.9 convolution_convert_fusion
  194.6 2.7 copy.83
  197.3 47.9 %reduce-scatter.3.cloned.1.call-done = bf16[1,1,6,8,3584]{4,2,3,1,0:T(8,128)(2,1)} async-done(((bf16[1,8,6,8,3584]{4,2,3,1,0:T(8,128)(2,1)}), bf16[1,1,6,8,3584]{4,2,3,1,0:T(8,128)(2,1)}) %reduce-scatter.3.cloned.1.call-update) | async-done | bytes 344080 | tf_op jit(solution)/shard_map/reduce_scatter | solution.py:69
  245.1 2.2 reshape.119
  247.3 14.8 %all-to-all-start.1 = ((bf16[1,8,168,128]{3,2,0,1:T(8,128)(2,1)}), bf16[1,8,168,128]{3,2,0,1:T(8,128)(2,1)S(1)}, u32[]{:S(2)}, u32[]{:S(2)}) async-start(bf16[1,8,168,128]{3,2,0,1:T(8,128)(2,1)} %bitcast.12), calls=%async_computation.2 | async-start | bytes 688128 | tf_op jit(solution)/shard_map/all_to_all | solution.py:72
  262.2 50.8 %reduce-scatter.5.cloned.1.call-done = bf16[1,1,6,8,3584]{4,2,3,1,0:T(8,128)(2,1)} async-done(((bf16[1,8,6,8,3584]{4,2,3,1,0:T(8,128)(2,1)}), bf16[1,1,6,8,3584]{4,2,3,1,0:T(8,128)(2,1)}) %reduce-scatter.5.cloned.1.call-update) | async-done | bytes 344080 | tf_op jit(solution)/shard_map/reduce_scatter | solution.py:69
  312.9 2.2 reshape.123
  315.1 13.2 %all-to-all-start.3 = ((bf16[1,8,168,128]{3,2,0,1:T(8,128)(2,1)}), bf16[1,8,168,128]{3,2,0,1:T(8,128)(2,1)S(1)}, u32[]{:S(2)}, u32[]{:S(2)}) async-start(bf16[1,8,168,128]{3,2,0,1:T(8,128)(2,1)} %bitcast.28), calls=%async_computation.5 | async-start | bytes 688128 | tf_op jit(solution)/shard_map/all_to_all | solution.py:72
  328.3 0.4 squeeze.41
  328.6 0.3 fusion
  328.9 3.3 collective-permute-start
  332.2 21.7 %all-to-all-done.3 = bf16[1,8,168,128]{3,2,0,1:T(8,128)(2,1)S(1)} async-done(((bf16[1,8,168,128]{3,2,0,1:T(8,128)(2,1)}), bf16[1,8,168,128]{3,2,0,1:T(8,128)(2,1)S(1)}, u32[]{:S(2)}, u32[]{:S(2)}) %all-to-all-start.3) | async-done | bytes 344096 | tf_op jit(solution)/shard_map/all_to_all | solution.py:72
  353.9 0.4 squeeze.47
  354.3 0.3 fusion.1
  354.6 3.4 collective-permute-start.1
  358.0 5.6 %collective-permute-done.1 = bf16[1,16,3584]{2,1,0:T(8,128)(2,1)S(1)} collective-permute-done((bf16[1,16,3584]{2,1,0:T(8,128)(2,1)S(1)}, bf16[1,16,3584]{2,1,0:T(8,128)(2,1)S(1)}, u32[]{:S(2)}, u32[]{:S(2)}) %collective-permute-start.1) | collective-permute-done | bytes 114720 | tf_op jit(solution)/shard_map/ppermute | solution.py:13
  363.6 0.6 copy.91
  364.3 0.6 copy.92
  (23 shorter events, 0.2 us)
Async XLA Ops:
  7.2 114.1 %copy-start = (bf16[1,128,3584]{2,1,0:T(8,128)(2,1)S(1)}, bf16[1,128,3584]{2,1,0:T(8,128)(2,1)}, u32[]{:S(2)}) copy-start(bf16[1,128,3584]{2,1,0:T(8,128)(2,1)} %param.19) | copy-start | bytes 2752516
  7.2 49.8 %copy-start.6 = (f32[1,16,2]{1,2,0:T(2,128)S(1)}, f32[1,16,2]{1,2,0:T(2,128)}, u32[]{:S(2)}) copy-start(f32[1,16,2]{1,2,0:T(2,128)} %param.15) | copy-start | bytes 388
  7.2 49.8 %copy-start.5 = (s32[1,16,2]{1,2,0:T(2,128)S(1)}, s32[1,16,2]{1,2,0:T(2,128)}, u32[]{:S(2)}) copy-start(s32[1,16,2]{1,2,0:T(2,128)} %param.14) | copy-start | bytes 388
  7.2 50.5 %copy-start.3 = (bf16[1,16,3584]{2,1,0:T(8,128)(2,1)S(1)}, bf16[1,16,3584]{2,1,0:T(8,128)(2,1)}, u32[]{:S(2)}) copy-start(bf16[1,16,3584]{2,1,0:T(8,128)(2,1)} %param.16) | copy-start | bytes 344068
  7.2 51.5 %copy-start.4 = (bf16[1,16,3584]{2,1,0:T(8,128)(2,1)S(1)}, bf16[1,16,3584]{2,1,0:T(8,128)(2,1)}, u32[]{:S(2)}) copy-start(bf16[1,16,3584]{2,1,0:T(8,128)(2,1)} %param.13) | copy-start | bytes 344068
  7.2 111.4 %all-gather.5.cloned.1.call-start = ((), (), s32[]{:S(2)}) async-start(), calls=%async_computation.8 | async-start | bytes 3096576 | tf_op jit(solution)/shard_map/all_gather | solution.py:64
  56.9 132.5 %all-gather.7.cloned.1.call-start = ((), (), s32[]{:S(2)}) async-start(), calls=%async_computation.9 | async-start | bytes 6193152 | tf_op jit(solution)/shard_map/all_gather | solution.py:64
  109.9 8.7 %copy-start.1 = (bf16[1,3584,128]{2,1,0:T(8,128)(2,1)S(1)}, bf16[1,3584,128]{2,1,0:T(8,128)(2,1)}, u32[]{:S(2)}) copy-start(bf16[1,3584,128]{2,1,0:T(8,128)(2,1)} %param.17) | copy-start | bytes 2752516
  111.8 9.5 %copy-start.2 = (bf16[1,3584,128]{2,1,0:T(8,128)(2,1)S(1)}, bf16[1,3584,128]{2,1,0:T(8,128)(2,1)}, u32[]{:S(2)}) copy-start(bf16[1,3584,128]{2,1,0:T(8,128)(2,1)} %param.18) | copy-start | bytes 2752516
  111.8 133.3 %reduce-scatter.3.cloned.1.call-start = ((), (), s32[]{:S(2)}) async-start(), calls=%async_computation.6 | async-start | bytes 4128768 | tf_op jit(solution)/shard_map/reduce_scatter | solution.py:69
  132.2 180.8 %reduce-scatter.5.cloned.1.call-start = ((), (), s32[]{:S(2)}) async-start(), calls=%async_computation.7 | async-start | bytes 4128768 | tf_op jit(solution)/shard_map/reduce_scatter | solution.py:69
  189.4 3.4 copy-start.7
  247.3 67.8 %all-to-all-start.1 = ((bf16[1,8,168,128]{3,2,0,1:T(8,128)(2,1)}), bf16[1,8,168,128]{3,2,0,1:T(8,128)(2,1)S(1)}, u32[]{:S(2)}, u32[]{:S(2)}) async-start(bf16[1,8,168,128]{3,2,0,1:T(8,128)(2,1)} %bitcast.12), calls=%async_computation.2 | async-start | bytes 688128 | tf_op jit(solution)/shard_map/all_to_all | solution.py:72
  315.1 38.8 %all-to-all-start.3 = ((bf16[1,8,168,128]{3,2,0,1:T(8,128)(2,1)}), bf16[1,8,168,128]{3,2,0,1:T(8,128)(2,1)S(1)}, u32[]{:S(2)}, u32[]{:S(2)}) async-start(bf16[1,8,168,128]{3,2,0,1:T(8,128)(2,1)} %bitcast.28), calls=%async_computation.5 | async-start | bytes 688128 | tf_op jit(solution)/shard_map/all_to_all | solution.py:72
  328.9 29.1 %collective-permute-start = (bf16[1,16,3584]{2,1,0:T(8,128)(2,1)S(1)}, bf16[1,16,3584]{2,1,0:T(8,128)(2,1)S(1)}, u32[]{:S(2)}, u32[]{:S(2)}) collective-permute-start(bf16[1,16,3584]{2,1,0:T(8,128)(2,1)S(1)} %fusion), channel_id=1, source_target_pairs={{0,64},{64,128},{128,192},{192,256},{256,320},{320,384},{384,448},... | collective-permute-start | bytes 344072 | tf_op jit(solution)/shard_map/ppermute | solution.py:13
  354.6 9.0 %collective-permute-start.1 = (bf16[1,16,3584]{2,1,0:T(8,128)(2,1)S(1)}, bf16[1,16,3584]{2,1,0:T(8,128)(2,1)S(1)}, u32[]{:S(2)}, u32[]{:S(2)}) collective-permute-start(bf16[1,16,3584]{2,1,0:T(8,128)(2,1)S(1)} %fusion.1), channel_id=1, source_target_pairs={{0,448},{64,0},{128,64},{192,128},{256,192},{320,256},{384,320},{4... | collective-permute-start | bytes 344072 | tf_op jit(solution)/shard_map/ppermute | solution.py:13
Sparse Core Ops, SparseCore 0:
  57.0 61.5 all-gather.4
  120.7 68.6 all-gather.6
  192.2 52.8 reduce-scatter.2
  247.8 65.0 reduce-scatter.4

commit v5 on v3

--- a/solution.py
+++ b/solution.py
@@ -93,7 +93,7 @@
     arrived = lax.all_gather(crossed, "ei", axis=1, tiled=False)
     rows = arrived.reshape(3, -1, width)
     parts = expert_pair(rows[:2].reshape(-1, width), rows[2], w_gate, w_up, w_down)
-    parts = parts.reshape((2,) + arrived.shape[1:])
+    parts = parts.reshape(2, arrived.shape[1], -1, width)
     summed = lax.psum_scatter(parts, "ei", scatter_dimension=1, tiled=True)
     summed = summed.reshape(2, capacity, experts, width).transpose(0, 2, 1, 3)
     summed = summed.reshape(2, experts, -1, lanes)

time: 364 us -> 345 us (0.948)
  waiting for transfers between devices: 182 us -> 165 us
    reduce_scatter x1, waiting for transfers between devices: 88.8 us -> 71.5 us  [body(): summed = lax.psum_scatter(parts, 'ei', scatter_dimension=1, tiled=True)]
where the time goes in v5:
time: 345 us; the launch traced here: 344 us
  waiting for transfers between devices  165 us (48%)
  blocking collectives  126 us (37%)
  local copies, waits for them, and re-layouts  18.7 us (5%)
  between operations  14.3 us (4%)
  matrix products  9.03 us (3%)
  starting transfers between devices  6.66 us (2%)
  other arithmetic  5.04 us (1%)
    all_gather x1, waiting for transfers between devices, body(): arrived = lax.all_gather(crossed, 'ei', axis=1, tiled=False)  86.4 us
    reduce_scatter x1, waiting for transfers between devices, body(): summed = lax.psum_scatter(parts, 'ei', scatter_dimension=1, tiled=True)  71.5 us
    all_to_all x1, blocking collectives, body(): lax.all_to_all(payload, 'eg', split_axis=1, concat_axis=1, tiled=True)  70.8 us
    all_to_all x1, blocking collectives, body(): home = lax.all_to_all(summed, 'eg', split_axis=1, concat_axis=1, tiled=True)  54.7 us
  transfers between devices with their start and end apart: 4, of which 4 were waited for; matrix products, arithmetic and copies ran while one was open for 0% of the time, Pallas kernels for 0%

profile of v5, /device:TPU:64, one launch (start us, length us, event | category | flops | bytes accessed | tf_op | source)
XLA Modules:
  0.0 344.1 jit_solution(16471375272318018901)
XLA Ops:
  7.2 0.0 copy-start
  7.2 0.0 all-gather.3.cloned.1.call-start
  7.2 0.8 copy.78
  8.0 0.1 eq.63
  8.1 0.1 fusion.30
  8.1 0.1 reduce_window_sum.18
  8.2 0.2 select_reduce_fusion.1
  8.4 0.1 reduce_sum.82
  8.5 0.1 copy.79
  8.6 0.7 bitcast_add_fusion
  9.3 0.7 reduce_sum.84
  10.0 0.7 bitcast_divide_fusion
  10.6 0.1 convert_reduce_fusion
  10.7 0.3 convolution_convert_fusion.2
  11.0 0.4 stack.13
  11.4 1.4 convolution_convert_fusion.1
  12.8 0.4 stack.14
  13.3 0.8 copy.76
  14.0 0.1 eq.56
  14.1 0.1 fusion.31
  14.2 0.1 reduce_window_sum.17
  14.3 0.2 select_reduce_fusion.3
  14.4 0.1 reduce_sum.77
  14.5 0.1 copy.77
  14.6 0.7 bitcast_add_fusion.1
  15.3 0.7 reduce_sum.78
  16.0 0.7 bitcast_divide_fusion.1
  16.7 0.1 convert_reduce_fusion.1
  16.8 1.2 convolution_convert_fusion.3
  17.9 0.4 stack.12
  18.4 0.1 pad_maximum_fusion
  18.5 70.8 %all_to_all.10 = bf16[3,8,168,128]{3,2,0,1:T(8,128)(2,1)S(1)} all-to-all(bf16[3,8,168,128]{3,2,0,1:T(8,128)(2,1)S(1)} %pad_maximum_fusion), channel_id=1, replica_groups=mesh['pipe'=8,'eg'=8,'ei'=8] {'eg'}, dimensions={1} | all-to-all | bytes 2064384 | tf_op jit(solution)/shard_map/all_to_all | solution.py:91
  89.4 0.1 copy.83
  89.5 1.2 reshape.102
  90.6 1.3 copy.84
  92.0 0.0 all-gather.3.cloned.1.call-update
  92.0 0.0 reduce-scatter.2.cloned.1.call-start
  92.1 0.5 copy.86
  92.6 0.5 copy.87
  93.1 86.4 %all-gather.3.cloned.1.call-done = bf16[3,48,8,3584]{3,2,0,1:T(8,128)(2,1)} async-done(((bf16[3,6,8,3584]{3,2,0,1:T(8,128)(2,1)}), bf16[3,48,8,3584]{3,2,0,1:T(8,128)(2,1)}) %all-gather.3.cloned.1.call-update) | async-done | bytes 8257552 | tf_op jit(solution)/shard_map/all_gather | solution.py:93
  179.5 2.6 slice-done.2
  182.1 0.4 copy.97
  182.5 1.6 fusion.8
  184.1 0.1 slice-done
  184.2 1.4 slice-done.1
  185.6 0.2 copy-done.3
  185.8 0.9 fusion.25
  186.7 3.2 convolution_convert_fusion
  189.9 2.7 copy.91
  192.7 0.0 reduce-scatter.2.cloned.1.call-update
  192.7 71.5 %reduce-scatter.2.cloned.1.call-done = bf16[2,1,48,3584]{3,2,0,1:T(8,128)(2,1)} async-done(((bf16[2,8,48,3584]{3,2,0,1:T(8,128)(2,1)}), bf16[2,1,48,3584]{3,2,0,1:T(8,128)(2,1)}) %reduce-scatter.2.cloned.1.call-update) | async-done | bytes 688144 | tf_op jit(solution)/shard_map/reduce_scatter | solution.py:97
  264.2 1.3 copy.95
  265.5 0.8 reshape.112
  266.3 54.7 %all_to_all.11 = bf16[2,8,168,128]{3,2,0,1:T(8,128)(2,1)S(1)} all-to-all(bf16[2,8,168,128]{3,2,0,1:T(8,128)(2,1)S(1)} %reshape.112), channel_id=1, replica_groups=mesh['pipe'=8,'eg'=8,'ei'=8] {'eg'}, dimensions={1} | all-to-all | bytes 1376256 | tf_op jit(solution)/shard_map/all_to_all | solution.py:100
  321.1 0.4 squeeze.43
  321.5 0.3 fusion.1
  321.8 4.7 %collective-permute-start.1 = (bf16[1,16,3584]{2,1,0:T(8,128)(2,1)S(1)}, bf16[1,16,3584]{2,1,0:T(8,128)(2,1)S(1)}, u32[]{:S(2)}, u32[]{:S(2)}) collective-permute-start(bf16[1,16,3584]{2,1,0:T(8,128)(2,1)S(1)} %fusion.1), channel_id=1, source_target_pairs={{0,448},{64,0},{128,64},{192,128},{256,192},{320,256},{384,320},{4... | collective-permute-start | bytes 344072 | tf_op jit(solution)/shard_map/ppermute | solution.py:13
  326.5 0.4 squeeze.42
  326.9 0.3 fusion
  327.1 1.9 collective-permute-start
  329.1 0.5 collective-permute-done.1
  329.6 6.4 %collective-permute-done = bf16[1,16,3584]{2,1,0:T(8,128)(2,1)S(1)} collective-permute-done((bf16[1,16,3584]{2,1,0:T(8,128)(2,1)S(1)}, bf16[1,16,3584]{2,1,0:T(8,128)(2,1)S(1)}, u32[]{:S(2)}, u32[]{:S(2)}) %collective-permute-start) | collective-permute-done | bytes 114720 | tf_op jit(solution)/shard_map/ppermute | solution.py:13
  335.9 0.6 copy.101
  336.6 0.6 copy.102
  (12 shorter events, 0.1 us)
Async XLA Ops:
  7.2 3.6 %copy-start = (bf16[1,16,3584]{2,1,0:T(8,128)(2,1)S(1)}, bf16[1,16,3584]{2,1,0:T(8,128)(2,1)}, u32[]{:S(2)}) copy-start(bf16[1,16,3584]{2,1,0:T(8,128)(2,1)} %param.13) | copy-start | bytes 344068
  7.2 172.3 %all-gather.3.cloned.1.call-start = ((), (), s32[]{:S(2)}) async-start(), calls=%async_computation.4 | async-start | bytes 9289728 | tf_op jit(solution)/shard_map/all_gather | solution.py:93
  89.4 2.6 copy-start.1
  90.6 2.0 copy-start.2
  92.0 172.2 %reduce-scatter.2.cloned.1.call-start = ((), (), s32[]{:S(2)}) async-start(), calls=%async_computation.3 | async-start | bytes 6193152 | tf_op jit(solution)/shard_map/reduce_scatter | solution.py:97
  179.5 2.6 slice-start.2
  182.1 2.2 slice-start
  182.5 3.1 slice-start.1
  182.5 3.3 copy-start.3
  321.8 7.8 %collective-permute-start.1 = (bf16[1,16,3584]{2,1,0:T(8,128)(2,1)S(1)}, bf16[1,16,3584]{2,1,0:T(8,128)(2,1)S(1)}, u32[]{:S(2)}, u32[]{:S(2)}) collective-permute-start(bf16[1,16,3584]{2,1,0:T(8,128)(2,1)S(1)} %fusion.1), channel_id=1, source_target_pairs={{0,448},{64,0},{128,64},{192,128},{256,192},{320,256},{384,320},{4... | collective-permute-start | bytes 344072 | tf_op jit(solution)/shard_map/ppermute | solution.py:13
  327.1 8.8 %collective-permute-start = (bf16[1,16,3584]{2,1,0:T(8,128)(2,1)S(1)}, bf16[1,16,3584]{2,1,0:T(8,128)(2,1)S(1)}, u32[]{:S(2)}, u32[]{:S(2)}) collective-permute-start(bf16[1,16,3584]{2,1,0:T(8,128)(2,1)S(1)} %fusion), channel_id=1, source_target_pairs={{0,64},{64,128},{128,192},{192,256},{256,320},{320,384},{384,448},... | collective-permute-start | bytes 344072 | tf_op jit(solution)/shard_map/ppermute | solution.py:13
Sparse Core Ops, SparseCore 0:
  92.1 87.3 all-gather.2
  192.8 71.3 reduce-scatter.1

commit v6 on v5

--- a/solution.py
+++ b/solution.py
@@ -77,7 +77,12 @@
     topk = fwd_routes.shape[2]
     width = fwd_tokens.shape[2]
     capacity = min(tokens, max(6, (tokens * topk + experts - 1) // experts + 2))
-    w_gate, w_up, w_down = gate_weight[0], up_weight[0], down_weight[0]
+    swap = [(0, 1), (1, 0)]
+    own = (gate_weight[0], up_weight[0], down_weight[0])
+    other = tuple(lax.ppermute(w, "c", swap) for w in own)
+    w_gate = jnp.concatenate((own[0], other[0]), axis=1)
+    w_up = jnp.concatenate((own[1], other[1]), axis=1)
+    w_down = jnp.concatenate((own[2], other[2]), axis=0)
     member_f, weight_f = route_tables(fwd_routes[0], fwd_scores[0], capacity, experts)
     member_b, weight_b = route_tables(bwd_routes[0], bwd_scores[0], capacity, experts)
     send_f = pick_rows(member_f, fwd_tokens[0])
@@ -90,11 +95,11 @@
     payload = jnp.stack((send_f, send_x, send_g)).reshape(3, experts, -1, lanes)
     crossed = lax.all_to_all(payload, "eg", split_axis=1, concat_axis=1, tiled=True)
     crossed = crossed.reshape(3, experts, capacity, width).transpose(0, 2, 1, 3)
-    arrived = lax.all_gather(crossed, "ei", axis=1, tiled=False)
+    arrived = lax.all_gather(crossed, "p", axis=1, tiled=False)
     rows = arrived.reshape(3, -1, width)
     parts = expert_pair(rows[:2].reshape(-1, width), rows[2], w_gate, w_up, w_down)
     parts = parts.reshape(2, arrived.shape[1], -1, width)
-    summed = lax.psum_scatter(parts, "ei", scatter_dimension=1, tiled=True)
+    summed = lax.psum_scatter(parts, "p", scatter_dimension=1, tiled=True)
     summed = summed.reshape(2, capacity, experts, width).transpose(0, 2, 1, 3)
     summed = summed.reshape(2, experts, -1, lanes)
     home = lax.all_to_all(summed, "eg", split_axis=1, concat_axis=1, tiled=True)
@@ -112,9 +117,10 @@
 
 def solution(mesh):
     pipe, expert = mesh.devices.shape
-    split = Mesh(mesh.devices.reshape(pipe, expert // GROUP, GROUP), ("pipe", "eg", "ei"))
-    rows = P("pipe", ("eg", "ei"), None)
-    cols = P("pipe", None, ("eg", "ei"))
+    shape = (pipe, expert // GROUP, GROUP // 2, 2)
+    split = Mesh(mesh.devices.reshape(shape), ("pipe", "eg", "p", "c"))
+    rows = P("pipe", ("eg", "p", "c"), None)
+    cols = P("pipe", None, ("eg", "p", "c"))
     placed = (rows, rows, rows, rows, rows, rows, rows, cols, cols, rows)
     return jax.shard_map(
         body,

time: 345 us -> 328 us (0.951)
  the two profiles are of different devices: /device:TPU:64 before, /device:TPU:96 now
where the time goes in v6:
time: 328 us; the launch traced here: 327 us
  waiting for transfers between devices  136 us (41%)
  blocking collectives  125 us (38%)
  local copies, waits for them, and re-layouts  18.8 us (6%)
  between operations  14.3 us (4%)
  starting transfers between devices  12.9 us (4%)
  matrix products  9.91 us (3%)
  other arithmetic  9.63 us (3%)
    all_to_all x1, blocking collectives, body(): lax.all_to_all(payload, 'eg', split_axis=1, concat_axis=1, tiled=True)  71 us
    reduce_scatter x1, waiting for transfers between devices, body(): summed = lax.psum_scatter(parts, 'p', scatter_dimension=1, tiled=True)  64.7 us
    all_gather x1, waiting for transfers between devices, body(): arrived = lax.all_gather(crossed, 'p', axis=1, tiled=False)  64.6 us
    all_to_all x1, blocking collectives, body(): home = lax.all_to_all(summed, 'eg', split_axis=1, concat_axis=1, tiled=True)  54 us
    ppermute x2, waiting for transfers between devices, from_behind(): return lax.ppermute(value, axis, pairs)  6.87 us
    ppermute x2, starting transfers between devices, from_behind(): return lax.ppermute(value, axis, pairs)  6.58 us
  transfers between devices with their start and end apart: 7, of which 4 were waited for; matrix products, arithmetic and copies ran while one was open for 2% of the time, Pallas kernels for 0%

profile of v6, /device:TPU:96, one launch (start us, length us, event | category | flops | bytes accessed | tf_op | source)
XLA Modules:
  0.0 326.9 jit_solution(16077947009322308374)
XLA Ops:
  7.2 0.8 copy.70
  8.0 0.1 eq.63
  8.1 0.1 fusion.39
  8.2 0.2 select_reduce_fusion.1
  8.4 0.1 reduce_sum.82
  8.5 0.1 copy.71
  8.6 0.7 bitcast_add_fusion
  9.3 0.7 reduce_sum.84
  10.0 0.7 bitcast_divide_fusion
  10.6 0.1 convert_reduce_fusion
  10.7 0.3 convolution_convert_fusion.2
  11.0 0.4 stack.13
  11.5 1.4 convolution_convert_fusion.1
  12.8 0.4 stack.14
  13.3 0.8 copy.68
  14.1 0.1 eq.56
  14.1 0.1 fusion.40
  14.2 0.1 reduce_window_sum.17
  14.3 0.2 select_reduce_fusion.3
  14.5 0.1 reduce_sum.77
  14.5 0.1 copy.69
  14.6 0.7 bitcast_add_fusion.1
  15.3 0.7 reduce_sum.78
  16.0 0.7 bitcast_divide_fusion.1
  16.7 0.1 convert_reduce_fusion.1
  16.8 1.2 convolution_convert_fusion.3
  18.0 0.4 stack.12
  18.4 0.1 pad_maximum_fusion
  18.5 71.0 %all_to_all.10 = bf16[3,8,168,128]{3,2,0,1:T(8,128)(2,1)S(1)} all-to-all(bf16[3,8,168,128]{3,2,0,1:T(8,128)(2,1)S(1)} %pad_maximum_fusion), channel_id=1, replica_groups=mesh['pipe'=8,'eg'=8,'p'=4,'c'=2] {'eg'}, dimensions={1} | all-to-all | bytes 2064384 | tf_op jit(solution)/shard_map/all_to_all | solution.py:96
  89.6 0.1 copy.75
  89.6 1.2 reshape.102
  90.8 1.3 copy.76
  92.2 1.9 collective-permute-start.2
  94.1 2.4 collective-permute-start
  96.6 1.9 collective-permute-start.1
  98.5 1.3 copy.79
  99.8 1.3 copy.80
  101.1 1.9 maximum_bitcast_fusion
  103.0 2.7 maximum_bitcast_fusion.1
  105.7 64.6 %all-gather.3.cloned.1.call-done = bf16[3,24,8,3584]{3,2,0,1:T(8,128)(2,1)} async-done(((bf16[3,6,8,3584]{3,2,0,1:T(8,128)(2,1)}), bf16[3,24,8,3584]{3,2,0,1:T(8,128)(2,1)}) %all-gather.3.cloned.1.call-update) | async-done | bytes 4128784 | tf_op jit(solution)/shard_map/all_gather | solution.py:98
  170.3 1.8 slice-done
  172.1 0.2 copy.86
  172.3 1.0 copy-done.4
  173.3 3.2 fusion.9
  176.6 0.8 fusion.34
  177.4 0.7 copy-done.2
  178.0 0.2 copy-done.9
  178.3 0.3 copy-done.10
  178.5 2.6 convolution_convert_fusion
  181.2 1.8 copy.81
  182.9 64.7 %reduce-scatter.2.cloned.1.call-done = bf16[2,1,48,3584]{3,2,0,1:T(8,128)(2,1)} async-done(((bf16[2,4,48,3584]{3,2,0,1:T(8,128)(2,1)}), bf16[2,1,48,3584]{3,2,0,1:T(8,128)(2,1)}) %reduce-scatter.2.cloned.1.call-update) | async-done | bytes 688144 | tf_op jit(solution)/shard_map/reduce_scatter | solution.py:102
  247.7 1.3 copy.84
  249.0 0.8 reshape.112
  249.9 54.0 %all_to_all.11 = bf16[2,8,168,128]{3,2,0,1:T(8,128)(2,1)S(1)} all-to-all(bf16[2,8,168,128]{3,2,0,1:T(8,128)(2,1)S(1)} %reshape.112), channel_id=1, replica_groups=mesh['pipe'=8,'eg'=8,'p'=4,'c'=2] {'eg'}, dimensions={1} | all-to-all | bytes 1376256 | tf_op jit(solution)/shard_map/all_to_all | solution.py:105
  303.9 0.4 squeeze.43
  304.4 0.3 fusion.8
  304.6 4.7 %collective-permute-start.4 = (bf16[1,16,3584]{2,1,0:T(8,128)(2,1)S(1)}, bf16[1,16,3584]{2,1,0:T(8,128)(2,1)S(1)}, u32[]{:S(2)}, u32[]{:S(2)}) collective-permute-start(bf16[1,16,3584]{2,1,0:T(8,128)(2,1)S(1)} %fusion.8), channel_id=1, source_target_pairs={{0,448},{64,0},{128,64},{192,128},{256,192},{320,256},{384,320},{4... | collective-permute-start | bytes 344072 | tf_op jit(solution)/shard_map/ppermute | solution.py:13
  309.3 0.4 squeeze.42
  309.7 0.3 fusion.7
  310.0 1.9 collective-permute-start.3
  311.9 0.4 collective-permute-done.4
  312.3 6.5 %collective-permute-done.3 = bf16[1,16,3584]{2,1,0:T(8,128)(2,1)S(1)} collective-permute-done((bf16[1,16,3584]{2,1,0:T(8,128)(2,1)S(1)}, bf16[1,16,3584]{2,1,0:T(8,128)(2,1)S(1)}, u32[]{:S(2)}, u32[]{:S(2)}) %collective-permute-start.3) | collective-permute-done | bytes 114720 | tf_op jit(solution)/shard_map/ppermute | solution.py:13
  318.7 0.6 copy.90
  319.4 0.6 copy.91
  (29 shorter events, 0.3 us)
Async XLA Ops:
  7.2 3.6 %copy-start = (bf16[1,16,3584]{2,1,0:T(8,128)(2,1)S(1)}, bf16[1,16,3584]{2,1,0:T(8,128)(2,1)}, u32[]{:S(2)}) copy-start(bf16[1,16,3584]{2,1,0:T(8,128)(2,1)} %param.13) | copy-start | bytes 344068
  7.2 163.2 %all-gather.3.cloned.1.call-start = ((), (), s32[]{:S(2)}) async-start(), calls=%async_computation.4 | async-start | bytes 5160960 | tf_op jit(solution)/shard_map/all_gather | solution.py:98
  89.6 7.0 %copy-start.3 = (bf16[1,3584,128]{2,1,0:T(8,128)(2,1)S(1)}, bf16[1,3584,128]{2,1,0:T(8,128)(2,1)}, u32[]{:S(2)}) copy-start(bf16[1,3584,128]{2,1,0:T(8,128)(2,1)} %param.18) | copy-start | bytes 2752516
  90.8 7.7 %copy-start.5 = (bf16[1,128,3584]{2,1,0:T(8,128)(2,1)S(1)}, bf16[1,128,3584]{2,1,0:T(8,128)(2,1)}, u32[]{:S(2)}) copy-start(bf16[1,128,3584]{2,1,0:T(8,128)(2,1)} %param.19) | copy-start | bytes 2752516
  92.1 155.6 %reduce-scatter.2.cloned.1.call-start = ((), (), s32[]{:S(2)}) async-start(), calls=%async_computation.3 | async-start | bytes 3440640 | tf_op jit(solution)/shard_map/reduce_scatter | solution.py:102
  92.2 7.6 %collective-permute-start.2 = (bf16[128,3584]{1,0:T(8,128)(2,1)}, bf16[128,3584]{1,0:T(8,128)(2,1)S(1)}, u32[]{:S(2)}, u32[]{:S(2)}) collective-permute-start(bf16[128,3584]{1,0:T(8,128)(2,1)} %bitcast.75), channel_id=1, source_target_pairs={{0,1},{1,0},{2,3},{3,2},{4,5},{5,4},{6,7},{7,6},{8,9},{9,8},{10,11... | collective-permute-start | bytes 2752520 | tf_op jit(solution)/shard_map/ppermute | solution.py:82
  94.1 7.0 %collective-permute-start = (bf16[3584,128]{1,0:T(8,128)(2,1)}, bf16[3584,128]{1,0:T(8,128)(2,1)}, u32[]{:S(2)}, u32[]{:S(2)}) collective-permute-start(bf16[3584,128]{1,0:T(8,128)(2,1)} %bitcast.72), channel_id=1, source_target_pairs={{0,1},{1,0},{2,3},{3,2},{4,5},{5,4},{6,7},{7,6},{8,9},{9,8},{10,11... | collective-permute-start | bytes 2752520 | tf_op jit(solution)/shard_map/ppermute | solution.py:82
  96.6 6.4 %collective-permute-start.1 = (bf16[3584,128]{1,0:T(8,128)(2,1)S(1)}, bf16[3584,128]{1,0:T(8,128)(2,1)}, u32[]{:S(2)}, u32[]{:S(2)}) collective-permute-start(bf16[3584,128]{1,0:T(8,128)(2,1)S(1)} %bitcast.69), channel_id=1, source_target_pairs={{0,1},{1,0},{2,3},{3,2},{4,5},{5,4},{6,7},{7,6},{8,9},{9,8},{10,11... | collective-permute-start | bytes 2752520 | tf_op jit(solution)/shard_map/ppermute | solution.py:82
  99.8 1.3 copy-start.7
  170.3 1.8 slice-start
  172.1 1.2 copy-start.4
  173.3 3.2 copy-start.1
  173.3 3.2 copy-start.6
  173.3 3.2 copy-start.8
  176.5 1.5 copy-start.2
  176.5 1.7 copy-start.9
  176.5 2.0 copy-start.10
  304.6 7.7 %collective-permute-start.4 = (bf16[1,16,3584]{2,1,0:T(8,128)(2,1)S(1)}, bf16[1,16,3584]{2,1,0:T(8,128)(2,1)S(1)}, u32[]{:S(2)}, u32[]{:S(2)}) collective-permute-start(bf16[1,16,3584]{2,1,0:T(8,128)(2,1)S(1)} %fusion.8), channel_id=1, source_target_pairs={{0,448},{64,0},{128,64},{192,128},{256,192},{320,256},{384,320},{4... | collective-permute-start | bytes 344072 | tf_op jit(solution)/shard_map/ppermute | solution.py:13
  310.0 8.8 %collective-permute-start.3 = (bf16[1,16,3584]{2,1,0:T(8,128)(2,1)S(1)}, bf16[1,16,3584]{2,1,0:T(8,128)(2,1)S(1)}, u32[]{:S(2)}, u32[]{:S(2)}) collective-permute-start(bf16[1,16,3584]{2,1,0:T(8,128)(2,1)S(1)} %fusion.7), channel_id=1, source_target_pairs={{0,64},{64,128},{128,192},{192,256},{256,320},{320,384},{384,448},... | collective-permute-start | bytes 344072 | tf_op jit(solution)/shard_map/ppermute | solution.py:13
Sparse Core Ops, SparseCore 0:
  92.3 78.0 all-gather.2
  183.1 64.5 reduce-scatter.1

commit v7 on v6

--- a/solution.py
+++ b/solution.py
@@ -14,17 +14,17 @@
 
 
 def route_tables(routes, scores, capacity, experts):
-    tokens, topk = routes.shape
-    flat = routes.reshape(-1)
-    onehot = (flat[:, None] == jnp.arange(experts, dtype=jnp.int32)[None, :]).astype(jnp.int32)
-    rank = jnp.cumsum(onehot, axis=0) - onehot
-    within = jnp.sum(rank * onehot, axis=1)
-    slot_ids = (flat * capacity + within).reshape(tokens, topk)
+    kinds, tokens, topk = routes.shape
+    flat = routes.reshape(kinds, -1)
+    onehot = (flat[:, :, None] == jnp.arange(experts, dtype=jnp.int32)).astype(jnp.int32)
+    rank = jnp.cumsum(onehot, axis=1) - onehot
+    within = jnp.sum(rank * onehot, axis=2)
+    slot_ids = (flat * capacity + within).reshape(kinds, tokens, topk)
     places = jnp.arange(experts * capacity, dtype=jnp.int32)
-    hits = (slot_ids[:, :, None] == places[None, None, :]).astype(jnp.float32)
-    normed = scores / jnp.sum(scores, axis=1, keepdims=True)
-    member = jnp.sum(hits, axis=1)
-    weighted = jnp.sum(hits * normed[:, :, None], axis=1)
+    hits = (slot_ids[..., None] == places).astype(jnp.float32)
+    normed = scores / jnp.sum(scores, axis=2, keepdims=True)
+    member = jnp.sum(hits, axis=2)
+    weighted = jnp.sum(hits * normed[..., None], axis=2)
     return (member, weighted)
 
 
@@ -83,16 +83,18 @@
     w_gate = jnp.concatenate((own[0], other[0]), axis=1)
     w_up = jnp.concatenate((own[1], other[1]), axis=1)
     w_down = jnp.concatenate((own[2], other[2]), axis=0)
-    member_f, weight_f = route_tables(fwd_routes[0], fwd_scores[0], capacity, experts)
-    member_b, weight_b = route_tables(bwd_routes[0], bwd_scores[0], capacity, experts)
-    send_f = pick_rows(member_f, fwd_tokens[0])
-    send_x = pick_rows(member_b, bwd_tokens[0])
-    route_grad = jnp.einsum(
-        "te,td->ed", weight_b, out_grad[0].astype(jnp.float32), precision=lax.Precision.HIGHEST
+    member, weighted = route_tables(
+        jnp.concatenate((fwd_routes, bwd_routes)),
+        jnp.concatenate((fwd_scores, bwd_scores)),
+        capacity,
+        experts,
     )
-    send_g = route_grad.astype(jnp.bfloat16)
+    weight_f, member_b = weighted[0], member[1]
+    pickers = jnp.stack((member[0], member_b, weighted[1]))
+    sources = jnp.concatenate((fwd_tokens, bwd_tokens, out_grad)).astype(jnp.float32)
+    chosen = jnp.einsum("kte,ktd->ked", pickers, sources, precision=lax.Precision.HIGHEST)
     lanes = 128
-    payload = jnp.stack((send_f, send_x, send_g)).reshape(3, experts, -1, lanes)
+    payload = chosen.astype(jnp.bfloat16).reshape(3, experts, -1, lanes)
     crossed = lax.all_to_all(payload, "eg", split_axis=1, concat_axis=1, tiled=True)
     crossed = crossed.reshape(3, experts, capacity, width).transpose(0, 2, 1, 3)
     arrived = lax.all_gather(crossed, "p", axis=1, tiled=False)

time: 328 us -> 323 us (0.985)
  other arithmetic: 9.63 us -> 5.07 us
where the time goes in v7:
time: 323 us
  waiting for transfers between devices  136 us (42%)
  blocking collectives  125 us (39%)
  local copies, waits for them, and re-layouts  19.8 us (6%)
  between operations  14.3 us (4%)
  starting transfers between devices  12.8 us (4%)
  matrix products  9.11 us (3%)
  other arithmetic  5.07 us (2%)
    all_to_all x1, blocking collectives, body(): lax.all_to_all(payload, 'eg', split_axis=1, concat_axis=1, tiled=True)  71 us
    reduce_scatter x1, waiting for transfers between devices, body(): summed = lax.psum_scatter(parts, 'p', scatter_dimension=1, tiled=True)  64.7 us
    all_gather x1, waiting for transfers between devices, body(): arrived = lax.all_gather(crossed, 'p', axis=1, tiled=False)  64.6 us
    all_to_all x1, blocking collectives, body(): home = lax.all_to_all(summed, 'eg', split_axis=1, concat_axis=1, tiled=True)  54.2 us
    ppermute x2, waiting for transfers between devices, from_behind(): return lax.ppermute(value, axis, pairs)  6.87 us
  transfers between devices with their start and end apart: 7, of which 4 were waited for; matrix products, arithmetic and copies ran while one was open for 2% of the time, Pallas kernels for 0%

profile of v7, /device:TPU:96, one launch (start us, length us, event | category | flops | bytes accessed | tf_op | source)
XLA Modules:
  0.0 322.5 jit_solution(6053573477972674119)
XLA Ops:
  7.2 0.0 all-gather.3.cloned.1.call-start
  7.2 0.7 constant_dynamic-update-slice_fusion.1
  7.9 0.7 constant_dynamic-update-slice_fusion
  8.6 0.1 copy.59
  8.7 0.1 eq.28
  8.8 0.1 fusion.41
  8.8 0.1 reduce_window_sum.11
  8.9 0.2 select_reduce_fusion.1
  9.1 0.1 reduce_sum.39
  9.2 0.1 copy.60
  9.3 0.7 constant_dynamic-update-slice_fusion.3
  10.0 0.7 constant_dynamic-update-slice_fusion.2
  10.7 0.1 convert_reduce_fusion
  10.8 2.0 convolution_convert_fusion.1
  12.8 1.3 reshape.63
  14.1 0.1 copy.61
  14.2 71.0 %all_to_all.10 = bf16[3,8,168,128]{3,2,0,1:T(8,128)(2,1)S(1)} all-to-all(bf16[3,8,168,128]{3,2,0,1:T(8,128)(2,1)S(1)} %copy.61), channel_id=1, replica_groups=mesh['pipe'=8,'eg'=8,'p'=4,'c'=2] {'eg'}, dimensions={1} | all-to-all | bytes 2064384 | tf_op jit(solution)/shard_map/all_to_all | solution.py:98
  85.2 0.1 copy.62
  85.3 1.2 reshape.64
  86.5 0.0 copy-start.4
  86.5 1.3 copy.63
  87.8 0.0 all-gather.3.cloned.1.call-update
  87.8 0.0 reduce-scatter.2.cloned.1.call-start
  87.8 1.9 collective-permute-start.2
  89.8 2.4 collective-permute-start
  92.2 0.0 copy-done.2
  92.2 1.9 collective-permute-start.1
  94.1 0.0 copy-done.4
  94.1 1.3 copy.66
  95.4 0.0 collective-permute-done.2
  95.4 1.3 copy.67
  96.7 0.0 copy-done.6
  96.8 0.0 collective-permute-done
  96.8 1.9 maximum_bitcast_fusion
  98.6 0.0 collective-permute-done.1
  98.6 2.7 maximum_bitcast_fusion.1
  101.4 64.6 %all-gather.3.cloned.1.call-done = bf16[3,24,8,3584]{3,2,0,1:T(8,128)(2,1)} async-done(((bf16[3,6,8,3584]{3,2,0,1:T(8,128)(2,1)}), bf16[3,24,8,3584]{3,2,0,1:T(8,128)(2,1)}) %all-gather.3.cloned.1.call-update) | async-done | bytes 4128784 | tf_op jit(solution)/shard_map/all_gather | solution.py:100
  166.0 1.8 slice-done
  167.8 0.2 copy.73
  168.0 1.0 copy-done.3
  169.0 3.2 fusion.9
  172.1 0.0 copy-done
  172.2 0.0 copy-done.7
  172.2 0.8 fusion.39
  173.0 0.7 copy-done.1
  173.7 0.2 copy-done.8
  173.9 0.3 copy-done.9
  174.2 2.6 convolution_convert_fusion
  176.8 1.7 copy.68
  178.6 0.0 reduce-scatter.2.cloned.1.call-update
  178.6 64.7 %reduce-scatter.2.cloned.1.call-done = bf16[2,1,48,3584]{3,2,0,1:T(8,128)(2,1)} async-done(((bf16[2,4,48,3584]{3,2,0,1:T(8,128)(2,1)}), bf16[2,1,48,3584]{3,2,0,1:T(8,128)(2,1)}) %reduce-scatter.2.cloned.1.call-update) | async-done | bytes 688144 | tf_op jit(solution)/shard_map/reduce_scatter | solution.py:104
  243.3 1.3 copy.71
  244.6 0.8 reshape.74
  245.5 54.2 %all_to_all.11 = bf16[2,8,168,128]{3,2,0,1:T(8,128)(2,1)S(1)} all-to-all(bf16[2,8,168,128]{3,2,0,1:T(8,128)(2,1)S(1)} %reshape.74), channel_id=1, replica_groups=mesh['pipe'=8,'eg'=8,'p'=4,'c'=2] {'eg'}, dimensions={1} | all-to-all | bytes 1376256 | tf_op jit(solution)/shard_map/all_to_all | solution.py:107
  299.7 0.4 squeeze.31
  300.1 0.3 fusion.8
  300.4 4.5 %collective-permute-start.4 = (bf16[1,16,3584]{2,1,0:T(8,128)(2,1)S(1)}, bf16[1,16,3584]{2,1,0:T(8,128)(2,1)S(1)}, u32[]{:S(2)}, u32[]{:S(2)}) collective-permute-start(bf16[1,16,3584]{2,1,0:T(8,128)(2,1)S(1)} %fusion.8), channel_id=1, source_target_pairs={{0,448},{64,0},{128,64},{192,128},{256,192},{320,256},{384,320},{4... | collective-permute-start | bytes 344072 | tf_op jit(solution)/shard_map/ppermute | solution.py:13
  304.9 0.4 squeeze.29
  305.3 0.3 fusion.7
  305.6 1.9 collective-permute-start.3
  307.5 0.4 collective-permute-done.4
  307.9 6.5 %collective-permute-done.3 = bf16[1,16,3584]{2,1,0:T(8,128)(2,1)S(1)} collective-permute-done((bf16[1,16,3584]{2,1,0:T(8,128)(2,1)S(1)}, bf16[1,16,3584]{2,1,0:T(8,128)(2,1)S(1)}, u32[]{:S(2)}, u32[]{:S(2)}) %collective-permute-start.3) | collective-permute-done | bytes 114720 | tf_op jit(solution)/shard_map/ppermute | solution.py:13
  314.4 0.6 copy.79
  315.0 0.6 copy.80
  (17 shorter events, 0.1 us)
Async XLA Ops:
  7.2 158.8 %all-gather.3.cloned.1.call-start = ((), (), s32[]{:S(2)}) async-start(), calls=%async_computation.4 | async-start | bytes 5160960 | tf_op jit(solution)/shard_map/all_gather | solution.py:100
  85.2 7.0 %copy-start.2 = (bf16[1,3584,128]{2,1,0:T(8,128)(2,1)S(1)}, bf16[1,3584,128]{2,1,0:T(8,128)(2,1)}, u32[]{:S(2)}) copy-start(bf16[1,3584,128]{2,1,0:T(8,128)(2,1)} %param.18) | copy-start | bytes 2752516
  86.5 7.7 %copy-start.4 = (bf16[1,128,3584]{2,1,0:T(8,128)(2,1)S(1)}, bf16[1,128,3584]{2,1,0:T(8,128)(2,1)}, u32[]{:S(2)}) copy-start(bf16[1,128,3584]{2,1,0:T(8,128)(2,1)} %param.19) | copy-start | bytes 2752516
  87.8 155.5 %reduce-scatter.2.cloned.1.call-start = ((), (), s32[]{:S(2)}) async-start(), calls=%async_computation.3 | async-start | bytes 3440640 | tf_op jit(solution)/shard_map/reduce_scatter | solution.py:104
  87.8 7.6 %collective-permute-start.2 = (bf16[128,3584]{1,0:T(8,128)(2,1)}, bf16[128,3584]{1,0:T(8,128)(2,1)S(1)}, u32[]{:S(2)}, u32[]{:S(2)}) collective-permute-start(bf16[128,3584]{1,0:T(8,128)(2,1)} %bitcast.54), channel_id=1, source_target_pairs={{0,1},{1,0},{2,3},{3,2},{4,5},{5,4},{6,7},{7,6},{8,9},{9,8},{10,11... | collective-permute-start | bytes 2752520 | tf_op jit(solution)/shard_map/ppermute | solution.py:82
  89.8 7.0 %collective-permute-start = (bf16[3584,128]{1,0:T(8,128)(2,1)}, bf16[3584,128]{1,0:T(8,128)(2,1)}, u32[]{:S(2)}, u32[]{:S(2)}) collective-permute-start(bf16[3584,128]{1,0:T(8,128)(2,1)} %bitcast.51), channel_id=1, source_target_pairs={{0,1},{1,0},{2,3},{3,2},{4,5},{5,4},{6,7},{7,6},{8,9},{9,8},{10,11... | collective-permute-start | bytes 2752520 | tf_op jit(solution)/shard_map/ppermute | solution.py:82
  92.2 6.4 %collective-permute-start.1 = (bf16[3584,128]{1,0:T(8,128)(2,1)S(1)}, bf16[3584,128]{1,0:T(8,128)(2,1)}, u32[]{:S(2)}, u32[]{:S(2)}) collective-permute-start(bf16[3584,128]{1,0:T(8,128)(2,1)S(1)} %bitcast.48), channel_id=1, source_target_pairs={{0,1},{1,0},{2,3},{3,2},{4,5},{5,4},{6,7},{7,6},{8,9},{9,8},{10,11... | collective-permute-start | bytes 2752520 | tf_op jit(solution)/shard_map/ppermute | solution.py:82
  95.4 1.3 copy-start.6
  166.0 1.8 slice-start
  167.8 1.2 copy-start.3
  169.0 3.2 copy-start
  169.0 3.2 copy-start.5
  169.0 3.2 %copy-start.7 = (bf16[128,3584]{1,0:T(8,128)(2,1)S(1)}, bf16[128,3584]{1,0:T(8,128)(2,1)}, u32[]{:S(2)}) copy-start(bf16[128,3584]{1,0:T(8,128)(2,1)} %copy-done.6) | copy-start | bytes 2752516
  172.2 1.5 copy-start.1
  172.2 1.7 copy-start.8
  172.2 2.0 copy-start.9
  300.4 7.5 %collective-permute-start.4 = (bf16[1,16,3584]{2,1,0:T(8,128)(2,1)S(1)}, bf16[1,16,3584]{2,1,0:T(8,128)(2,1)S(1)}, u32[]{:S(2)}, u32[]{:S(2)}) collective-permute-start(bf16[1,16,3584]{2,1,0:T(8,128)(2,1)S(1)} %fusion.8), channel_id=1, source_target_pairs={{0,448},{64,0},{128,64},{192,128},{256,192},{320,256},{384,320},{4... | collective-permute-start | bytes 344072 | tf_op jit(solution)/shard_map/ppermute | solution.py:13
  305.6 8.8 %collective-permute-start.3 = (bf16[1,16,3584]{2,1,0:T(8,128)(2,1)S(1)}, bf16[1,16,3584]{2,1,0:T(8,128)(2,1)S(1)}, u32[]{:S(2)}, u32[]{:S(2)}) collective-permute-start(bf16[1,16,3584]{2,1,0:T(8,128)(2,1)S(1)} %fusion.7), channel_id=1, source_target_pairs={{0,64},{64,128},{128,192},{192,256},{256,320},{320,384},{384,448},... | collective-permute-start | bytes 344072 | tf_op jit(solution)/shard_map/ppermute | solution.py:13
Sparse Core Ops, SparseCore 0:
  87.9 78.0 all-gather.2
  178.7 64.5 reduce-scatter.1

commit v8 on v7

--- a/solution.py
+++ b/solution.py
@@ -35,16 +35,22 @@
     return slots.astype(jnp.bfloat16)
 
 
-def expert_pair(rows, grads, w_gate, w_up, w_down):
+def expert_pair(mixed, grads, w_gate, w_up, w_down):
     count = grads.shape[0]
     hid = w_gate.shape[1]
-    both = jnp.dot(rows, jnp.concatenate((w_gate, w_up), axis=1), preferred_element_type=jnp.float32)
-    first, second = both[:, :hid], both[:, hid:]
-    hidden = (jax.nn.silu(first[:count]) * second[:count]).astype(jnp.bfloat16)
+    width = mixed.shape[-1]
+    both = jnp.dot(
+        mixed.reshape(-1, width),
+        jnp.concatenate((w_gate, w_up), axis=1),
+        preferred_element_type=jnp.float32,
+    ).reshape(mixed.shape[:3] + (2 * hid,))
+    fwd = both[:, 0].reshape(count, 2 * hid)
+    bwd = both[:, 1].reshape(count, 2 * hid)
+    hidden = (jax.nn.silu(fwd[:, :hid]) * fwd[:, hid:]).astype(jnp.bfloat16)
     d_hidden = lax.dot_general(
         grads, w_down, (((1,), (1,)), ((), ())), preferred_element_type=jnp.float32
     )
-    a, b = first[count:], second[count:]
+    a, b = bwd[:, :hid], bwd[:, hid:]
     sigm = 1.0 / (1.0 + jnp.exp(-a))
     d_first = (d_hidden * b * sigm * (1.0 + a * (1.0 - sigm))).astype(jnp.bfloat16)
     d_second = (d_hidden * a * sigm).astype(jnp.bfloat16)
@@ -99,7 +105,8 @@
     crossed = crossed.reshape(3, experts, capacity, width).transpose(0, 2, 1, 3)
     arrived = lax.all_gather(crossed, "p", axis=1, tiled=False)
     rows = arrived.reshape(3, -1, width)
-    parts = expert_pair(rows[:2].reshape(-1, width), rows[2], w_gate, w_up, w_down)
+    mixed = arrived.transpose(1, 2, 0, 3, 4).reshape(-1, 3, experts, width)
+    parts = expert_pair(mixed, rows[2], w_gate, w_up, w_down)
     parts = parts.reshape(2, arrived.shape[1], -1, width)
     summed = lax.psum_scatter(parts, "p", scatter_dimension=1, tiled=True)
     summed = summed.reshape(2, capacity, experts, width).transpose(0, 2, 1, 3)

time: 323 us -> 324 us (level)
  local copies, waits for them, and re-layouts: 19.8 us -> 14.4 us
  matrix products: 9.11 us -> 14.1 us
  transfers between devices with their start and end apart: 7 -> 7, of which waited for: 4 -> 4; matrix products, arithmetic and copies ran while one was open for 2% -> 4% of each run, Pallas kernels for 0% -> 0%
where the time goes in v8:
time: 324 us; the launch traced here: 323 us
  waiting for transfers between devices  138 us (43%)
  blocking collectives  125 us (39%)
  local copies, waits for them, and re-layouts  14.4 us (4%)
  between operations  14.3 us (4%)
  matrix products  14.1 us (4%)
  starting transfers between devices  12.9 us (4%)
  other arithmetic  5.06 us (2%)
    all_to_all x1, blocking collectives, body(): lax.all_to_all(payload, 'eg', split_axis=1, concat_axis=1, tiled=True)  71 us
    all_gather x1, waiting for transfers between devices, body(): arrived = lax.all_gather(crossed, 'p', axis=1, tiled=False)  66 us
    reduce_scatter x1, waiting for transfers between devices, body(): summed = lax.psum_scatter(parts, 'p', scatter_dimension=1, tiled=True)  64.7 us
    all_to_all x1, blocking collectives, body(): home = lax.all_to_all(summed, 'eg', split_axis=1, concat_axis=1, tiled=True)  54 us
    ppermute x2, waiting for transfers between devices, from_behind(): return lax.ppermute(value, axis, pairs)  6.87 us
    ppermute x2, starting transfers between devices, from_behind(): return lax.ppermute(value, axis, pairs)  6.58 us
  transfers between devices with their start and end apart: 7, of which 4 were waited for; matrix products, arithmetic and copies ran while one was open for 4% of the time, Pallas kernels for 0%

profile of v8, /device:TPU:96, one launch (start us, length us, event | category | flops | bytes accessed | tf_op | source)
XLA Modules:
  0.0 323.5 jit_solution(14386879256726746175)
XLA Ops:
  7.2 0.0 all-gather.3.cloned.1.call-start
  7.2 0.7 constant_dynamic-update-slice_fusion.1
  7.9 0.7 constant_dynamic-update-slice_fusion
  8.6 0.1 copy.70
  8.7 0.1 eq.28
  8.8 0.1 fusion.41
  8.8 0.1 reduce_window_sum.11
  8.9 0.2 select_reduce_fusion.1
  9.1 0.1 reduce_sum.39
  9.2 0.1 copy.71
  9.3 0.7 constant_dynamic-update-slice_fusion.3
  10.0 0.7 constant_dynamic-update-slice_fusion.2
  10.7 0.1 convert_reduce_fusion
  10.8 2.0 convolution_convert_fusion.1
  12.8 1.3 reshape.61
  14.1 0.1 copy.72
  14.2 71.0 %all_to_all.10 = bf16[3,8,168,128]{3,2,0,1:T(8,128)(2,1)S(1)} all-to-all(bf16[3,8,168,128]{3,2,0,1:T(8,128)(2,1)S(1)} %copy.72), channel_id=1, replica_groups=mesh['pipe'=8,'eg'=8,'p'=4,'c'=2] {'eg'}, dimensions={1} | all-to-all | bytes 2064384 | tf_op jit(solution)/shard_map/all_to_all | solution.py:104
  85.2 0.0 copy-start.1
  85.2 0.1 copy.73
  85.3 1.2 reshape.62
  86.5 0.0 copy-start.2
  86.5 1.3 copy.74
  87.8 0.0 all-gather.3.cloned.1.call-update
  87.8 0.0 reduce-scatter.2.cloned.1.call-start
  87.9 1.9 collective-permute-start
  89.8 0.0 copy-done.1
  89.8 2.4 collective-permute-start.1
  92.2 0.0 copy-done.2
  92.2 1.3 copy.78
  93.5 1.9 collective-permute-start.2
  95.4 0.0 collective-permute-done
  95.4 1.8 maximum_bitcast_fusion.2
  97.3 0.0 collective-permute-done.1
  97.3 2.7 maximum_bitcast_fusion.3
  100.0 66.0 %all-gather.3.cloned.1.call-done = bf16[3,24,8,3584]{3,2,0,1:T(8,128)(2,1)} async-done(((bf16[3,6,8,3584]{3,2,0,1:T(8,128)(2,1)}), bf16[3,24,8,3584]{3,2,0,1:T(8,128)(2,1)}) %all-gather.3.cloned.1.call-update) | async-done | bytes 4128784 | tf_op jit(solution)/shard_map/all_gather | solution.py:106
  166.0 5.3 %fusion.9 = f32[24,3,8,512]{3,2,1,0:T(8,128)S(1)} fusion(bf16[3,24,8,3584]{3,2,0,1:T(8,128)(2,1)} %all-gather.3.cloned.1.call-done, bf16[3584,128]{1,0:T(8,128)(2,1)} %collective-permute-done.1, bf16[3584,128]{1,0:T(8,128)(2,1)S(1)} %bitcast.63, bf16[3584,128]{1,0:T(8,128)(2,1)} %collective-permute-done, bf16[3584,128]{1,0:T(8,128)(2,1)} %bitcast.66), kind=kOutput, calls=%fused_computation.13 | convolution fusion | flops 2128609280 | bytes 8978432 | tf_op jit(solution)/shard_map/dot_general | solution.py:42
  171.3 0.1 slice_bitcast_fusion.2
  171.3 0.1 fusion.40
  171.4 0.0 collective-permute-done.2
  171.4 0.0 copy-start
  171.4 2.5 fusion.39
  174.0 0.0 copy-done
  174.0 3.8 %convolution_convert_fusion = bf16[384,3584]{1,0:T(8,128)(2,1)S(1)} fusion(bf16[256,3584]{0,1:T(8,128)(2,1)S(1)} %copy-done, bf16[256,3584]{0,1:T(8,128)(2,1)S(1)} %maximum_bitcast_fusion.2, bf16[128,3584]{0,1:T(8,128)(2,1)} %collective-permute-done.2, bf16[128,3584]{0,1:T(8,128)(2,1)} %bitcast.12, bf16[192,256]{1,0:T(8,128)(2,1)S(1)} %fusion.40, ...), kind=kOutput, calls=%fused_computation | convolution fusion | flops 2140274688 | bytes 8650752 | tf_op jit(solution)/shard_map/dot_general | solution.py:66
  177.8 1.8 copy.79
  179.5 0.0 reduce-scatter.2.cloned.1.call-update
  179.6 64.7 %reduce-scatter.2.cloned.1.call-done = bf16[2,1,48,3584]{3,2,0,1:T(8,128)(2,1)} async-done(((bf16[2,4,48,3584]{3,2,0,1:T(8,128)(2,1)}), bf16[2,1,48,3584]{3,2,0,1:T(8,128)(2,1)}) %reduce-scatter.2.cloned.1.call-update) | async-done | bytes 688144 | tf_op jit(solution)/shard_map/reduce_scatter | solution.py:111
  244.3 1.3 copy.84
  245.6 0.8 reshape.70
  246.5 54.0 %all_to_all.11 = bf16[2,8,168,128]{3,2,0,1:T(8,128)(2,1)S(1)} all-to-all(bf16[2,8,168,128]{3,2,0,1:T(8,128)(2,1)S(1)} %reshape.70), channel_id=1, replica_groups=mesh['pipe'=8,'eg'=8,'p'=4,'c'=2] {'eg'}, dimensions={1} | all-to-all | bytes 1376256 | tf_op jit(solution)/shard_map/all_to_all | solution.py:114
  300.5 0.4 squeeze.31
  300.9 0.3 fusion.8
  301.2 4.7 %collective-permute-start.4 = (bf16[1,16,3584]{2,1,0:T(8,128)(2,1)S(1)}, bf16[1,16,3584]{2,1,0:T(8,128)(2,1)S(1)}, u32[]{:S(2)}, u32[]{:S(2)}) collective-permute-start(bf16[1,16,3584]{2,1,0:T(8,128)(2,1)S(1)} %fusion.8), channel_id=1, source_target_pairs={{0,448},{64,0},{128,64},{192,128},{256,192},{320,256},{384,320},{4... | collective-permute-start | bytes 344072 | tf_op jit(solution)/shard_map/ppermute | solution.py:13
  305.9 0.4 squeeze.29
  306.3 0.3 fusion.7
  306.5 1.9 collective-permute-start.3
  308.5 0.4 collective-permute-done.4
  308.9 6.4 %collective-permute-done.3 = bf16[1,16,3584]{2,1,0:T(8,128)(2,1)S(1)} collective-permute-done((bf16[1,16,3584]{2,1,0:T(8,128)(2,1)S(1)}, bf16[1,16,3584]{2,1,0:T(8,128)(2,1)S(1)}, u32[]{:S(2)}, u32[]{:S(2)}) %collective-permute-start.3) | collective-permute-done | bytes 114720 | tf_op jit(solution)/shard_map/ppermute | solution.py:13
  315.3 0.6 copy.91
  316.0 0.6 copy.92
  (6 shorter events, 0.1 us)
Async XLA Ops:
  7.2 158.8 %all-gather.3.cloned.1.call-start = ((), (), s32[]{:S(2)}) async-start(), calls=%async_computation.4 | async-start | bytes 5160960 | tf_op jit(solution)/shard_map/all_gather | solution.py:106
  85.2 4.6 %copy-start.1 = (bf16[1,3584,128]{2,1,0:T(8,128)(2,1)S(1)}, bf16[1,3584,128]{2,1,0:T(8,128)(2,1)}, u32[]{:S(2)}) copy-start(bf16[1,3584,128]{2,1,0:T(8,128)(2,1)} %param.18) | copy-start | bytes 2752516
  86.5 5.7 %copy-start.2 = (bf16[1,128,3584]{2,1,0:T(8,128)(2,1)S(1)}, bf16[1,128,3584]{2,1,0:T(8,128)(2,1)}, u32[]{:S(2)}) copy-start(bf16[1,128,3584]{2,1,0:T(8,128)(2,1)} %param.19) | copy-start | bytes 2752516
  87.8 156.5 %reduce-scatter.2.cloned.1.call-start = ((), (), s32[]{:S(2)}) async-start(), calls=%async_computation.3 | async-start | bytes 3440640 | tf_op jit(solution)/shard_map/reduce_scatter | solution.py:111
  87.9 7.6 %collective-permute-start = (bf16[3584,128]{1,0:T(8,128)(2,1)}, bf16[3584,128]{1,0:T(8,128)(2,1)}, u32[]{:S(2)}, u32[]{:S(2)}) collective-permute-start(bf16[3584,128]{1,0:T(8,128)(2,1)} %bitcast.64), channel_id=1, source_target_pairs={{0,1},{1,0},{2,3},{3,2},{4,5},{5,4},{6,7},{7,6},{8,9},{9,8},{10,11... | collective-permute-start | bytes 2752520 | tf_op jit(solution)/shard_map/ppermute | solution.py:88
  89.8 7.5 %collective-permute-start.1 = (bf16[3584,128]{1,0:T(8,128)(2,1)S(1)}, bf16[3584,128]{1,0:T(8,128)(2,1)}, u32[]{:S(2)}, u32[]{:S(2)}) collective-permute-start(bf16[3584,128]{1,0:T(8,128)(2,1)S(1)} %bitcast.61), channel_id=1, source_target_pairs={{0,1},{1,0},{2,3},{3,2},{4,5},{5,4},{6,7},{7,6},{8,9},{9,8},{10,11... | collective-permute-start | bytes 2752520 | tf_op jit(solution)/shard_map/ppermute | solution.py:88
  93.5 77.9 %collective-permute-start.2 = (bf16[128,3584]{0,1:T(8,128)(2,1)}, bf16[128,3584]{0,1:T(8,128)(2,1)}, u32[]{:S(2)}, u32[]{:S(2)}) collective-permute-start(bf16[128,3584]{0,1:T(8,128)(2,1)} %bitcast.12), channel_id=1, source_target_pairs={{0,1},{1,0},{2,3},{3,2},{4,5},{5,4},{6,7},{7,6},{8,9},{9,8},{10,11... | collective-permute-start | bytes 2752520 | tf_op jit(solution)/shard_map/ppermute | solution.py:88
  171.4 2.6 copy-start
  301.2 7.7 %collective-permute-start.4 = (bf16[1,16,3584]{2,1,0:T(8,128)(2,1)S(1)}, bf16[1,16,3584]{2,1,0:T(8,128)(2,1)S(1)}, u32[]{:S(2)}, u32[]{:S(2)}) collective-permute-start(bf16[1,16,3584]{2,1,0:T(8,128)(2,1)S(1)} %fusion.8), channel_id=1, source_target_pairs={{0,448},{64,0},{128,64},{192,128},{256,192},{320,256},{384,320},{4... | collective-permute-start | bytes 344072 | tf_op jit(solution)/shard_map/ppermute | solution.py:13
  306.5 8.8 %collective-permute-start.3 = (bf16[1,16,3584]{2,1,0:T(8,128)(2,1)S(1)}, bf16[1,16,3584]{2,1,0:T(8,128)(2,1)S(1)}, u32[]{:S(2)}, u32[]{:S(2)}) collective-permute-start(bf16[1,16,3584]{2,1,0:T(8,128)(2,1)S(1)} %fusion.7), channel_id=1, source_target_pairs={{0,64},{64,128},{128,192},{192,256},{256,320},{320,384},{384,448},... | collective-permute-start | bytes 344072 | tf_op jit(solution)/shard_map/ppermute | solution.py:13
Sparse Core Ops, SparseCore 0:
  87.9 78.0 all-gather.2
  179.7 64.5 reduce-scatter.1

commit v9 on v7

--- a/solution.py
+++ b/solution.py
@@ -57,7 +57,10 @@
         axis=0,
     )
     right = jnp.concatenate((w_down, w_gate.T, w_up.T), axis=0)
-    return jnp.dot(left, right, preferred_element_type=jnp.float32).astype(jnp.bfloat16)
+    chips = lax.axis_size("p")
+    left = left.reshape(2, chips, -1, left.shape[-1]).transpose(1, 0, 2, 3).reshape(left.shape)
+    out = jnp.dot(left, right, preferred_element_type=jnp.float32).astype(jnp.bfloat16)
+    return out.reshape(chips, 2, -1, out.shape[-1]).transpose(1, 0, 2, 3).reshape(out.shape)
 
 
 def body(

time: 323 us -> 322 us (level)
  no operation moved by 1% of the time
where the time goes in v9:
time: 322 us
  waiting for transfers between devices  136 us (42%)
  blocking collectives  125 us (39%)
  local copies, waits for them, and re-layouts  18 us (6%)
  between operations  14.3 us (4%)
  starting transfers between devices  12.9 us (4%)
  matrix products  10.2 us (3%)
  other arithmetic  5.11 us (2%)
    all_to_all x1, blocking collectives, body(): lax.all_to_all(payload, 'eg', split_axis=1, concat_axis=1, tiled=True)  71 us
    reduce_scatter x1, waiting for transfers between devices, body(): summed = lax.psum_scatter(parts, 'p', scatter_dimension=1, tiled=True)  64.7 us
    all_gather x1, waiting for transfers between devices, body(): arrived = lax.all_gather(crossed, 'p', axis=1, tiled=False)  64.6 us
    all_to_all x1, blocking collectives, body(): home = lax.all_to_all(summed, 'eg', split_axis=1, concat_axis=1, tiled=True)  54 us
    ppermute x2, waiting for transfers between devices, from_behind(): return lax.ppermute(value, axis, pairs)  6.87 us
    ppermute x2, starting transfers between devices, from_behind(): return lax.ppermute(value, axis, pairs)  6.6 us
  transfers between devices with their start and end apart: 7, of which 4 were waited for; matrix products, arithmetic and copies ran while one was open for 2% of the time, Pallas kernels for 0%

profile of v9, /device:TPU:96, one launch (start us, length us, event | category | flops | bytes accessed | tf_op | source)
XLA Modules:
  0.0 321.9 jit_solution(3616313622085528260)
XLA Ops:
  7.2 0.0 all-gather.3.cloned.1.call-start
  7.2 0.7 constant_dynamic-update-slice_fusion.1
  7.9 0.7 constant_dynamic-update-slice_fusion
  8.6 0.1 copy.60
  8.7 0.1 eq.28
  8.8 0.1 fusion.32
  8.8 0.1 reduce_window_sum.11
  8.9 0.2 select_reduce_fusion.1
  9.1 0.1 reduce_sum.39
  9.2 0.1 copy.61
  9.3 0.7 constant_dynamic-update-slice_fusion.3
  10.0 0.7 constant_dynamic-update-slice_fusion.2
  10.7 0.1 convert_reduce_fusion
  10.8 2.0 convolution_convert_fusion.1
  12.8 1.3 reshape.69
  14.1 0.1 copy.62
  14.2 71.0 %all_to_all.10 = bf16[3,8,168,128]{3,2,0,1:T(8,128)(2,1)S(1)} all-to-all(bf16[3,8,168,128]{3,2,0,1:T(8,128)(2,1)S(1)} %copy.62), channel_id=1, replica_groups=mesh['pipe'=8,'eg'=8,'p'=4,'c'=2] {'eg'}, dimensions={1} | all-to-all | bytes 2064384 | tf_op jit(solution)/shard_map/all_to_all | solution.py:101
  85.2 0.1 copy.63
  85.3 1.2 reshape.70
  86.5 0.0 copy-start.4
  86.5 1.3 copy.64
  87.8 0.0 all-gather.3.cloned.1.call-update
  87.8 0.0 reduce-scatter.2.cloned.1.call-start
  87.8 1.9 collective-permute-start.2
  89.8 2.4 collective-permute-start
  92.2 0.0 copy-done.2
  92.2 1.9 collective-permute-start.1
  94.1 0.0 copy-done.4
  94.1 1.3 copy.68
  95.4 0.0 collective-permute-done.2
  95.4 1.3 copy.69
  96.7 0.0 copy-done.8
  96.8 0.0 collective-permute-done
  96.8 1.9 maximum_bitcast_fusion
  98.6 0.0 collective-permute-done.1
  98.6 2.7 maximum_bitcast_fusion.1
  101.4 64.6 %all-gather.3.cloned.1.call-done = bf16[3,24,8,3584]{3,2,0,1:T(8,128)(2,1)} async-done(((bf16[3,6,8,3584]{3,2,0,1:T(8,128)(2,1)}), bf16[3,24,8,3584]{3,2,0,1:T(8,128)(2,1)}) %all-gather.3.cloned.1.call-update) | async-done | bytes 4128784 | tf_op jit(solution)/shard_map/all_gather | solution.py:103
  166.0 1.8 slice-done
  167.8 0.2 copy.74
  168.0 1.0 copy-done.3
  169.0 3.2 fusion.9
  172.1 0.0 copy-done
  172.2 0.0 copy-done.5
  172.2 0.0 copy-done.9
  172.2 0.8 fusion.30
  173.1 0.6 copy-done.1
  173.7 0.2 copy-done.6
  173.9 0.3 copy-done.7
  174.2 3.7 %convolution_convert_fusion = bf16[384,3584]{1,0:T(8,128)(2,1)} fusion(bf16[384,768]{1,0:T(8,128)(2,1)S(1)} %bitcast.66, bf16[256,3584]{0,1:T(8,128)(2,1)S(1)} %copy-done.1, bf16[256,3584]{0,1:T(8,128)(2,1)S(1)} %maximum_bitcast_fusion, bf16[128,3584]{0,1:T(8,128)(2,1)S(1)} %copy-done.7, bf16[128,3584]{0,1:T(8,128)(2,1)S(1)} %copy-done.6), kind=kOutput, calls=%fused_computation | convolution fusion | flops 2137325568 | bytes 8847360 | tf_op jit(solution)/shard_map/dot_general | solution.py:62
  177.9 0.0 reduce-scatter.2.cloned.1.call-update
  177.9 64.7 %reduce-scatter.2.cloned.1.call-done = bf16[2,1,48,3584]{3,2,0,1:T(8,128)(2,1)} async-done(((bf16[2,4,48,3584]{3,2,0,1:T(8,128)(2,1)}), bf16[2,1,48,3584]{3,2,0,1:T(8,128)(2,1)}) %reduce-scatter.2.cloned.1.call-update) | async-done | bytes 688144 | tf_op jit(solution)/shard_map/reduce_scatter | solution.py:107
  242.7 1.3 copy.72
  244.0 0.8 reshape.82
  244.8 54.0 %all_to_all.11 = bf16[2,8,168,128]{3,2,0,1:T(8,128)(2,1)S(1)} all-to-all(bf16[2,8,168,128]{3,2,0,1:T(8,128)(2,1)S(1)} %reshape.82), channel_id=1, replica_groups=mesh['pipe'=8,'eg'=8,'p'=4,'c'=2] {'eg'}, dimensions={1} | all-to-all | bytes 1376256 | tf_op jit(solution)/shard_map/all_to_all | solution.py:110
  298.9 0.4 squeeze.31
  299.3 0.3 fusion.8
  299.6 4.7 %collective-permute-start.4 = (bf16[1,16,3584]{2,1,0:T(8,128)(2,1)S(1)}, bf16[1,16,3584]{2,1,0:T(8,128)(2,1)S(1)}, u32[]{:S(2)}, u32[]{:S(2)}) collective-permute-start(bf16[1,16,3584]{2,1,0:T(8,128)(2,1)S(1)} %fusion.8), channel_id=1, source_target_pairs={{0,448},{64,0},{128,64},{192,128},{256,192},{320,256},{384,320},{4... | collective-permute-start | bytes 344072 | tf_op jit(solution)/shard_map/ppermute | solution.py:13
  304.3 0.4 squeeze.29
  304.7 0.3 fusion.7
  304.9 1.9 collective-permute-start.3
  306.9 0.4 collective-permute-done.4
  307.2 6.5 %collective-permute-done.3 = bf16[1,16,3584]{2,1,0:T(8,128)(2,1)S(1)} collective-permute-done((bf16[1,16,3584]{2,1,0:T(8,128)(2,1)S(1)}, bf16[1,16,3584]{2,1,0:T(8,128)(2,1)S(1)}, u32[]{:S(2)}, u32[]{:S(2)}) %collective-permute-start.3) | collective-permute-done | bytes 114720 | tf_op jit(solution)/shard_map/ppermute | solution.py:13
  313.7 0.6 copy.80
  314.4 0.6 copy.81
  (18 shorter events, 0.2 us)
Async XLA Ops:
  7.2 158.8 %all-gather.3.cloned.1.call-start = ((), (), s32[]{:S(2)}) async-start(), calls=%async_computation.4 | async-start | bytes 5160960 | tf_op jit(solution)/shard_map/all_gather | solution.py:103
  85.2 7.0 %copy-start.2 = (bf16[1,3584,128]{2,1,0:T(8,128)(2,1)S(1)}, bf16[1,3584,128]{2,1,0:T(8,128)(2,1)}, u32[]{:S(2)}) copy-start(bf16[1,3584,128]{2,1,0:T(8,128)(2,1)} %param.18) | copy-start | bytes 2752516
  86.5 7.7 %copy-start.4 = (bf16[1,128,3584]{2,1,0:T(8,128)(2,1)S(1)}, bf16[1,128,3584]{2,1,0:T(8,128)(2,1)}, u32[]{:S(2)}) copy-start(bf16[1,128,3584]{2,1,0:T(8,128)(2,1)} %param.19) | copy-start | bytes 2752516
  87.8 154.9 %reduce-scatter.2.cloned.1.call-start = ((), (), s32[]{:S(2)}) async-start(), calls=%async_computation.3 | async-start | bytes 3440640 | tf_op jit(solution)/shard_map/reduce_scatter | solution.py:107
  87.8 7.6 %collective-permute-start.2 = (bf16[128,3584]{1,0:T(8,128)(2,1)}, bf16[128,3584]{1,0:T(8,128)(2,1)S(1)}, u32[]{:S(2)}, u32[]{:S(2)}) collective-permute-start(bf16[128,3584]{1,0:T(8,128)(2,1)} %bitcast.62), channel_id=1, source_target_pairs={{0,1},{1,0},{2,3},{3,2},{4,5},{5,4},{6,7},{7,6},{8,9},{9,8},{10,11... | collective-permute-start | bytes 2752520 | tf_op jit(solution)/shard_map/ppermute | solution.py:85
  89.8 7.0 %collective-permute-start = (bf16[3584,128]{1,0:T(8,128)(2,1)}, bf16[3584,128]{1,0:T(8,128)(2,1)}, u32[]{:S(2)}, u32[]{:S(2)}) collective-permute-start(bf16[3584,128]{1,0:T(8,128)(2,1)} %bitcast.59), channel_id=1, source_target_pairs={{0,1},{1,0},{2,3},{3,2},{4,5},{5,4},{6,7},{7,6},{8,9},{9,8},{10,11... | collective-permute-start | bytes 2752520 | tf_op jit(solution)/shard_map/ppermute | solution.py:85
  92.2 6.4 %collective-permute-start.1 = (bf16[3584,128]{1,0:T(8,128)(2,1)S(1)}, bf16[3584,128]{1,0:T(8,128)(2,1)}, u32[]{:S(2)}, u32[]{:S(2)}) collective-permute-start(bf16[3584,128]{1,0:T(8,128)(2,1)S(1)} %bitcast.56), channel_id=1, source_target_pairs={{0,1},{1,0},{2,3},{3,2},{4,5},{5,4},{6,7},{7,6},{8,9},{9,8},{10,11... | collective-permute-start | bytes 2752520 | tf_op jit(solution)/shard_map/ppermute | solution.py:85
  95.4 1.3 copy-start.8
  166.0 1.8 slice-start
  167.8 1.2 copy-start.3
  169.0 3.2 copy-start
  169.0 3.2 copy-start.5
  169.0 3.2 %copy-start.9 = (bf16[128,3584]{1,0:T(8,128)(2,1)S(1)}, bf16[128,3584]{1,0:T(8,128)(2,1)}, u32[]{:S(2)}) copy-start(bf16[128,3584]{1,0:T(8,128)(2,1)} %copy-done.8) | copy-start | bytes 2752516
  172.2 1.5 copy-start.1
  172.2 1.7 copy-start.6
  172.2 2.0 copy-start.7
  299.6 7.7 %collective-permute-start.4 = (bf16[1,16,3584]{2,1,0:T(8,128)(2,1)S(1)}, bf16[1,16,3584]{2,1,0:T(8,128)(2,1)S(1)}, u32[]{:S(2)}, u32[]{:S(2)}) collective-permute-start(bf16[1,16,3584]{2,1,0:T(8,128)(2,1)S(1)} %fusion.8), channel_id=1, source_target_pairs={{0,448},{64,0},{128,64},{192,128},{256,192},{320,256},{384,320},{4... | collective-permute-start | bytes 344072 | tf_op jit(solution)/shard_map/ppermute | solution.py:13
  304.9 8.8 %collective-permute-start.3 = (bf16[1,16,3584]{2,1,0:T(8,128)(2,1)S(1)}, bf16[1,16,3584]{2,1,0:T(8,128)(2,1)S(1)}, u32[]{:S(2)}, u32[]{:S(2)}) collective-permute-start(bf16[1,16,3584]{2,1,0:T(8,128)(2,1)S(1)} %fusion.7), channel_id=1, source_target_pairs={{0,64},{64,128},{128,192},{192,256},{256,320},{320,384},{384,448},... | collective-permute-start | bytes 344072 | tf_op jit(solution)/shard_map/ppermute | solution.py:13
Sparse Core Ops, SparseCore 0:
  87.9 78.0 all-gather.2
  178.0 64.5 reduce-scatter.1
